TPU v7x, 32 devices: a whole 2x2x4 slice. The times are simulated.
32 devices in a mesh: row: 4 (over z), col: 8 (over y, x, core).
Axes of the slice: x: 2, y: 2, z: 4, core: 2. Of those that a mesh axis runs over, the one named last changes fastest.
Arguments:
- covariance: float32 [8192, 8192], P('row', 'col'), as said below
- self_block: bfloat16 [8192, 512], P(('row', 'col')), may hold values from -0.25 to 0.25
- wake_block: bfloat16 [16, 4, 128, 128], replicated, may hold values from -0.375 to 0.375
- upstream: int32 [16, 4], replicated, may hold values from -1 to 15, as said below
- process_noise: float32 [8192], P('col'), may hold values from 0.5 to 2
- sensor_turbine: int32 [384], replicated, may hold values from 0 to 15
- azimuth_index: int32 [16], replicated, may hold values from 0 to 71
- sensor_weight: float32 [384, 512], replicated, may hold values from -0.25 to 0.25
- sensor_noise: float32 [384], replicated, may hold values from 0.5 to 2
Outputs:
- posterior: float32 [8192, 8192], P('row', 'col')
- kalman_gain: float32 [8192, 384], P('row', 'col')
Inputs may be any that keep to these rules, and one draw needn't show every extreme that they name: Row t lists distinct turbines other than t that lie upstream of t, valid entries first, then -1; some turbine lists 4. `covariance`: symmetric and positive definite.
All inputs are finite; a program needn't handle non-finite values.
Results may differ from a plain program's by a relative error of at most 0.0048.
Values may be sent and summed in bfloat16 or wider, within the bound.
No kernel may reach another device: no remote copies, remote signals or barrier semaphores. Data moves between devices by JAX's collectives and lax.ppermute only.
A program may use at most 128 MiB of HBM per device.

v0:
```python
import math

import jax
import jax.numpy as jnp
from jax import lax
from jax.sharding import PartitionSpec as P

TURB = 16
SPT = 512
INF = 128
NUP = 4
NAZ = 72


def broadcast(value, axis, root):
    mine = lax.axis_index(axis) == root
    return lax.psum(jnp.where(mine, value, jnp.zeros_like(value)), axis)


def observe_columns(sensor_weight, sensor_turbine, azimuth_index, start, count):
    sensors = sensor_weight.shape[0]
    matches = sensor_turbine[:, None] == jnp.arange(TURB)[None, :]
    rotor_index = jnp.sum(jnp.where(matches, azimuth_index[None, :], 0), axis=1)
    sensor_index = jnp.arange(sensors)
    blade_angle = rotor_index.astype(jnp.float32) * jnp.float32(2.0 * math.pi / NAZ) + (
        sensor_index % 3
    ).astype(jnp.float32) * jnp.float32(2.0 * math.pi / 3.0)
    positions = start + jnp.arange(count)
    turbine_of = positions // SPT
    offset_of = positions % SPT
    widened = jnp.tile(sensor_weight, (1, max(1, count // SPT)))
    weights = lax.dynamic_slice_in_dim(widened, start % SPT, count, 1)
    cosine = jnp.cos(blade_angle)[:, None]
    sine = jnp.sin(blade_angle)[:, None]
    factor = jnp.where(
        offset_of[None, :] < 2 * INF,
        jnp.float32(1.0),
        jnp.where(offset_of[None, :] < 3 * INF, cosine, sine),
    )
    return jnp.where(
        sensor_turbine[:, None] == turbine_of[None, :], weights * factor, jnp.float32(0.0)
    )


def transition_strip(target_rows, wake_block, upstream, start, count):
    positions = start + jnp.arange(count)
    turbine_of = positions // SPT
    offset_of = positions % SPT
    turbine_ids = jnp.arange(TURB)
    own_match = turbine_of[:, None] == turbine_ids[None, :]
    self_part = jnp.where(
        own_match[:, :, None], target_rows[:, None, :], jnp.zeros((), jnp.bfloat16)
    )
    flat_wake = wake_block.reshape(TURB * NUP * INF, INF)
    coupling = jnp.zeros((count, TURB, INF), jnp.bfloat16)
    for slot_index in range(NUP):
        anchor = jnp.sum(jnp.where(own_match, upstream[None, :, slot_index], 0), axis=1)
        lookup = (turbine_of * NUP + slot_index) * INF + jnp.minimum(offset_of, INF - 1)
        coefficient = jnp.take(flat_wake, lookup, axis=0)
        usable = (offset_of < INF) & (anchor >= 0)
        source_match = (anchor[:, None] == turbine_ids[None, :]) & usable[:, None]
        coupling = coupling + jnp.where(
            source_match[:, :, None], coefficient[:, None, :], jnp.zeros((), jnp.bfloat16)
        )
    strip = jnp.concatenate([self_part[:, :, :INF] + coupling, self_part[:, :, INF:]], 2)
    return strip.reshape(count, TURB * SPT)


def shards(
    covariance,
    self_block,
    wake_block,
    upstream,
    process_noise,
    sensor_turbine,
    azimuth_index,
    sensor_weight,
    sensor_noise,
):
    row_count, col_count = covariance.shape
    row_start = lax.axis_index("row") * row_count
    col_start = lax.axis_index("col") * col_count
    per_row = row_count // SPT
    first_turbine = lax.axis_index("row") * per_row
    source_rows = lax.all_gather(covariance, "row", axis=0, tiled=True)
    row_stride = SPT
    own_rows = lax.all_gather(self_block, "col", axis=0, tiled=True)
    blocks = []
    for local in range(per_row):
        turbine = first_turbine + local
        diag_rows = own_rows[local * SPT : (local + 1) * SPT].astype(jnp.float32)
        own_source = covariance[local * SPT : (local + 1) * SPT]
        result = jnp.dot(diag_rows, own_source, precision=lax.Precision.HIGHEST)
        inflow_sum = jnp.zeros((INF, col_count), jnp.float32)
        for slot_index in range(NUP):
            anchor = upstream[turbine, slot_index]
            start_row = jnp.maximum(anchor, 0) * row_stride
            piece = lax.dynamic_slice_in_dim(source_rows, start_row, INF, 0)
            coupling = wake_block[turbine, slot_index].astype(jnp.float32)
            term = jnp.dot(coupling, piece, precision=lax.Precision.HIGHEST)
            inflow_sum = inflow_sum + jnp.where(anchor >= 0, term, jnp.float32(0.0))
        result = result + jnp.concatenate(
            [inflow_sum, jnp.zeros((SPT - INF, col_count), jnp.float32)], 0
        )
        blocks.append(result)
    half_product = jnp.concatenate(blocks, 0).astype(jnp.bfloat16)
    target_rows = lax.dynamic_slice_in_dim(own_rows, col_start % row_count, col_count, 0)
    target_rows = broadcast(target_rows, "row", col_start // row_count)
    strip = transition_strip(target_rows, wake_block, upstream, col_start, col_count)
    predicted = lax.dot_general(
        lax.all_gather(half_product, "col", axis=1, tiled=True),
        strip,
        (((1,), (1,)), ((), ())),
        preferred_element_type=jnp.float32,
    )
    row_ids = row_start + jnp.arange(row_count)
    col_ids = col_start + jnp.arange(col_count)
    predicted = predicted + jnp.where(
        row_ids[:, None] == col_ids[None, :], process_noise[None, :], jnp.float32(0.0)
    )
    col_observe = observe_columns(
        sensor_weight, sensor_turbine, azimuth_index, col_start, col_count
    )
    partial_cross = jnp.dot(predicted, col_observe.T, precision=lax.Precision.HIGHEST)
    cross_cov = lax.psum(partial_cross, "col")
    row_observe = observe_columns(
        sensor_weight, sensor_turbine, azimuth_index, row_start, row_count
    )
    partial_innovation = jnp.dot(row_observe, cross_cov, precision=lax.Precision.HIGHEST)
    innovation = lax.psum(partial_innovation, "row") + jnp.diag(sensor_noise)
    symmetric = 0.5 * (innovation + innovation.T)
    lower = jnp.linalg.cholesky(symmetric)
    gain_block = jax.scipy.linalg.cho_solve((lower, True), cross_cov.T).T
    target_cross = lax.dynamic_slice_in_dim(cross_cov, col_start % row_count, col_count, 0)
    target_cross = broadcast(target_cross, "row", col_start // row_count)
    posterior = predicted - jnp.dot(gain_block, target_cross.T, precision=lax.Precision.HIGHEST)
    share = gain_block.shape[1] // lax.axis_size("col")
    gain_share = lax.dynamic_slice_in_dim(gain_block, lax.axis_index("col") * share, share, 1)
    return (posterior, gain_share)


def solution(mesh):
    in_specs = (P("row", "col"), P(("row", "col"), None), P(), P(), P("col"), P(), P(), P(), P())
    out_specs = (P("row", "col"), P("row", "col"))
    return jax.shard_map(shards, mesh=mesh, in_specs=in_specs, out_specs=out_specs, check_vma=False)
```

profile of v0, /device:TPU:0, one launch (start us, length us, event | category | flops | bytes accessed | tf_op | source)
XLA Modules:
  0.0 1200.7 jit_solution(1399222346441279778)
XLA Ops:
  29.8 10.7 all-gather.4.cloned.1.call-done
  43.0 560.5 %all-gather.6.cloned.1.call-done = f32[8192,1024]{1,0:T(8,128)} async-done(((f32[2048,1024]{1,0:T(8,128)}), f32[8192,1024]{1,0:T(8,128)}) %all-gather.6.cloned.1.call-update) | async-done | bytes 33554448 | tf_op jit(solution)/shard_map/all_gather | solution.py:85
  610.0 3.6 add_convert_fusion.2
  646.2 4.3 gather_fusion.1
  650.6 4.3 gather_fusion
  661.2 6.7 broadcast_select_fusion
  671.2 10.0 slice_add_fusion
  683.7 13.7 %copy.33 = bf16[128,8,16,512]{3,1,2,0:T(8,128)(2,1)} copy(bf16[128,8,16,512]{3,2,1,0:T(8,128)(2,1)S(1)} %bitcast.154) | data formatting | bytes 33554432
  697.4 121.3 %all-gather.8.cloned.1.call-done = bf16[2048,8192]{1,0:T(8,128)(2,1)} async-done(((bf16[2048,1024]{1,0:T(8,128)(2,1)}), bf16[2048,8192]{1,0:T(8,128)(2,1)}) %all-gather.8.cloned.1.call-update) | async-done | bytes 33554448 | tf_op jit(solution)/shard_map/all_gather | solution.py:111
  818.7 40.8 %fusion.196 = f32[2048,1024]{1,0:T(8,128)S(1)} fusion(bf16[2048,8192]{1,0:T(8,128)(2,1)} %all-gather.8.cloned.1.call-done, bf16[1024,8192]{1,0:T(8,128)(2,1)} %bitcast.157), kind=kOutput, calls=%fused_computation.325 | convolution fusion | flops 34359738368 | bytes 58720256 | tf_op jit(solution)/shard_map/dot_general | solution.py:110
  859.6 3.4 copy-done.2
  863.0 15.8 %fusion.1 = f32[2048,384]{1,0:T(8,128)} fusion(f32[2048,1024]{1,0:T(8,128)S(1)} %fusion.196, f32[1024]{0:T(1024)S(1)} %copy-done.13, s32[1024]{0:T(1024)S(1)} %copy-done.11, s32[2048]{0:T(1024)S(1)} %iota_add_fusion, f32[384,1024]{1,0:T(8,128)S(1)} %bitcast.166, f32[384]{0:T(512)S(1)} %copy-done.15, f32[384]{0:T(512)S(1)} %copy-done.14, ...), kind=kOutput, calls=%fused_computation.10 | convolution fusion | flops 9671933952 | bytes 13134336 | tf_op jit(solution)/shard_map/dot_general | solution.py:124
  882.8 65.7 %all-reduce.12.cloned.1.call-done = f32[2048,384]{1,0:T(8,128)} async-done(((f32[2048,384]{1,0:T(8,128)}), f32[2048,384]{1,0:T(8,128)}) %all-reduce.12.cloned.1.call-update) | async-done | bytes 3145744 | tf_op jit(solution)/shard_map/psum | solution.py:125
  951.3 8.8 fusion.6
  960.1 89.8 %all-reduce.14.cloned.1.call-done = (f32[1024,384]{1,0:T(8,128)}, f32[384,384]{0,1:T(8,128)}) async-done(((f32[1024,384]{1,0:T(8,128)}, f32[384,384]{0,1:T(8,128)}), (f32[1024,384]{1,0:T(8,128)}, f32[384,384]{0,1:T(8,128)})) %all-reduce.14.cloned.1.call-update) | async-done | bytes 2162704 | tf_op jit(solution)/shard_map/psum | solution.py:17
  1052.7 12.2 %cholesky.76 = f32[128,128]{1,0:T(8,128)S(1)} custom-call(f32[128,128]{1,0:T(8,128)S(1)} %cholesky.189), custom_call_target="Cholesky" | custom-call | tf_op jit(solution)/shard_map/jit(cholesky)/cholesky | solution.py:132
  1064.9 9.8 custom-call.26
  1075.3 11.7 cholesky.160
  1087.3 9.8 custom-call.27
  1097.9 11.9 cholesky.179
  1113.9 6.4 while.1
  1120.3 29.5 %custom-call.28 = f32[3,128,128]{1,2,0:T(8,128)S(1)} custom-call(f32[3,128,128]{2,1,0:T(8,128)S(1)} %get-tuple-element.10), custom_call_target="InvertDiagBlocksLowerTriangular" | custom-call | tf_op jit(solution)/shard_map/jit(_cho_solve)/triangular_solve | solution.py:133
  1156.2 4.7 convolution_subtract_fusion.1
  1169.0 23.7 %fusion = f32[2048,1024]{1,0:T(8,128)} fusion(f32[2048,1024]{1,0:T(8,128)S(1)} %bitcast.160, f32[1024,384]{1,0:T(8,128)S(1)} %copy-done.6, f32[1024]{0:T(1024)S(1)} %copy-done.13, s32[1024]{0:T(1024)S(1)} %copy-done.11, s32[2048]{0:T(1024)S(1)} %iota_add_fusion, f32[128,2048]{1,0:T(8,128)S(1)} %fusion.109, f32[128,2048]{1,0:T(8,128)S(1)} %fusion.107, ...), kind=kOutput, calls=%fused_computation.9 | convolution fusion | flops 9673637888 | bytes 21512192 | tf_op jit(solution)/shard_map/dot_general | solution.py:136
  (176 shorter events, 90.4 us)
Async XLA Ops:
  7.2 596.4 %copy-start = (bf16[16,4,128,128]{3,2,1,0:T(8,128)(2,1)S(1)}, bf16[16,4,128,128]{3,2,1,0:T(8,128)(2,1)}, u32[]{:S(2)}) copy-start(bf16[16,4,128,128]{3,2,1,0:T(8,128)(2,1)} %param.13) | copy-start | bytes 6291460
  7.2 33.4 %all-gather.4.cloned.1.call-start = ((), (), s32[]{:S(2)}) async-start(), calls=%async_computation | async-start | bytes 2359296 | tf_op jit(solution)/shard_map/all_gather | solution.py:87
  7.9 595.6 %all-gather.6.cloned.1.call-start = ((), (), s32[]{:S(2)}) async-start(), calls=%async_computation.1 | async-start | bytes 41943040 | tf_op jit(solution)/shard_map/all_gather | solution.py:85
  8.7 652.6 %all-reduce.10.cloned.1.call-start = ((), (), s32[]{:S(2)}) async-start(), calls=%async_computation.3 | async-start | bytes 2097152 | tf_op jit(solution)/shard_map/psum | solution.py:17
  43.0 775.7 %all-gather.8.cloned.1.call-start = ((), (), s32[]{:S(2)}) async-start(), calls=%async_computation.2 | async-start | bytes 37748736 | tf_op jit(solution)/shard_map/all_gather | solution.py:111
  603.6 6.4 copy-start.4
  603.6 15.9 %slice-start = ((s8[8388608]{0:T(1024)(128)(4,1)}), s8[4194304]{0:T(1024)(128)(4,1)S(1)}, s32[]{:S(2)}) async-start(s8[8388608]{0:T(1024)(128)(4,1)} %bitcast.155), calls=%async_computation.6 | async-start | bytes 8388608
  609.9 9.5 slice-start.1
  639.4 309.1 %all-reduce.12.cloned.1.call-start = ((), (), s32[]{:S(2)}) async-start(), calls=%async_computation.4 | async-start | bytes 6291456 | tf_op jit(solution)/shard_map/psum | solution.py:125
  643.0 11.8 copy-start.5
  654.8 6.0 copy-start.9
  655.4 5.6 copy-start.8
  818.7 44.3 %copy-start.7 = (f32[48,8,2,512]{3,1,2,0:T(8,128)S(1)}, f32[48,8,2,512]{3,1,2,0:T(8,128)}, u32[]{:S(2)}) copy-start(f32[48,8,2,512]{3,1,2,0:T(8,128)} %copy.35) | copy-start | bytes 4718596
  818.7 44.3 %copy-start.11 = (s32[1024]{0:T(1024)S(1)}, s32[1024]{0:T(1024)}, u32[]{:S(2)}) copy-start(s32[1024]{0:T(1024)} %iota_add_fusion.1) | copy-start | bytes 12292
  818.7 44.3 %copy-start.13 = (f32[1024]{0:T(1024)S(1)}, f32[1024]{0:T(1024)}, u32[]{:S(2)}) copy-start(f32[1024]{0:T(1024)} %param.15) | copy-start | bytes 12292
  818.7 44.3 %copy-start.14 = (f32[384]{0:T(512)S(1)}, f32[384]{0:T(512)}, u32[]{:S(2)}) copy-start(f32[384]{0:T(512)} %get-tuple-element.39) | copy-start | bytes 4612
  818.7 44.3 %copy-start.15 = (f32[384]{0:T(512)S(1)}, f32[384]{0:T(512)}, u32[]{:S(2)}) copy-start(f32[384]{0:T(512)} %get-tuple-element.40) | copy-start | bytes 4612
  818.7 44.3 %copy-start.17 = (s32[384]{0:T(512)S(1)}, s32[384]{0:T(512)}, u32[]{:S(2)}) copy-start(s32[384]{0:T(512)} %param.16) | copy-start | bytes 4612
  818.7 44.3 %copy-start.18 = (pred[1024]{0:T(1024)(128)(4,1)S(1)}, pred[1024]{0:T(1024)(128)(4,1)}, u32[]{:S(2)}) copy-start(pred[1024]{0:T(1024)(128)(4,1)} %get-tuple-element.75) | copy-start | bytes 3076
  818.7 44.3 %copy-start.19 = (pred[1024]{0:T(1024)(128)(4,1)S(1)}, pred[1024]{0:T(1024)(128)(4,1)}, u32[]{:S(2)}) copy-start(pred[1024]{0:T(1024)(128)(4,1)} %get-tuple-element.76) | copy-start | bytes 3076
  878.8 171.0 %all-reduce.14.cloned.1.call-start = ((), (), s32[]{:S(2)}) async-start(), calls=%async_computation.5 | async-start | bytes 4325376 | tf_op jit(solution)/shard_map/psum | solution.py:17
  951.3 98.6 %copy-start.12 = (f32[384]{0:T(512)S(1)}, f32[384]{0:T(512)}, u32[]{:S(2)}) copy-start(f32[384]{0:T(512)} %param.19) | copy-start | bytes 4612
  1163.0 5.0 slice-start.2
  1169.0 24.5 %copy-start.1 = (bf16[16,4,128,128]{3,2,1,0:T(8,128)(2,1)S(1)}, bf16[16,4,128,128]{3,2,1,0:T(8,128)(2,1)}, u32[]{:S(2)}) copy-start(bf16[16,4,128,128]{3,2,1,0:T(8,128)(2,1)} %param.13) | copy-start | bytes 6291460
  (7 other events, 17.9 us)
Sparse Core Ops, SparseCore 0:
  9.9 30.6 all-gather.3
  42.1 561.4 all-gather.5
  605.9 50.0 all-reduce.9
  658.5 160.1 all-gather.7
  879.0 69.4 all-reduce.11
  960.2 89.6 all-reduce.13
where the time goes:
time: 1210 us; the launch traced here: 1200 us
  waiting for transfers between devices  849 us (70%)
  matrix products  141 us (12%)
  other arithmetic  121 us (10%)
  local copies, waits for them, and re-layouts  51 us (4%)
  between operations  37.6 us (3%)
    all_gather x1, waiting for transfers between devices, shards(): source_rows = lax.all_gather(covariance, 'row', axis=0, tiled=True)  561 us
    all_gather x1, waiting for transfers between devices, shards(): lax.all_gather(half_product, 'col', axis=1, tiled=True)  121 us
    psum x2, waiting for transfers between devices, broadcast(): return lax.psum(jnp.where(mine, value, jnp.zeros_like(value)), axis)  89.8 us
    psum x1, waiting for transfers between devices, shards(): cross_cov = lax.psum(partial_cross, 'col')  65.7 us
    another operation x11, other arithmetic, shards(): lower = jnp.linalg.cholesky(symmetric)  57.4 us
    dot_general x1, matrix products, shards(): lax.dot_general(lax.all_gather(half_product, 'col', axis=1, tiled=True),...  40.8 us
    another operation x4, other arithmetic, shards(): gain_block = jax.scipy.linalg.cho_solve((lower, True), cross_cov.T).T  29.9 us
  transfers between devices with their start and end apart: 6, of which 5 were waited for; matrix products, arithmetic and copies ran while one was open for 8% of the time, Pallas kernels for 0%

commit v1 on v0

v1 whole, which is shorter than its diff:
```python
import math

import jax
import jax.numpy as jnp
from jax import lax
from jax.sharding import PartitionSpec as P

TURB = 16
SPT = 512
INF = 128
NUP = 4
NAZ = 72


def broadcast(value, axis, root):
    mine = lax.axis_index(axis) == root
    return lax.psum(jnp.where(mine, value, jnp.zeros_like(value)), axis)


def observe_columns(sensor_weight, sensor_turbine, azimuth_index, start, count):
    sensors = sensor_weight.shape[0]
    matches = sensor_turbine[:, None] == jnp.arange(TURB)[None, :]
    rotor_index = jnp.sum(jnp.where(matches, azimuth_index[None, :], 0), axis=1)
    sensor_index = jnp.arange(sensors)
    blade_angle = rotor_index.astype(jnp.float32) * jnp.float32(2.0 * math.pi / NAZ) + (
        sensor_index % 3
    ).astype(jnp.float32) * jnp.float32(2.0 * math.pi / 3.0)
    positions = start + jnp.arange(count)
    turbine_of = positions // SPT
    offset_of = positions % SPT
    widened = jnp.tile(sensor_weight, (1, max(1, count // SPT)))
    weights = lax.dynamic_slice_in_dim(widened, start % SPT, count, 1)
    cosine = jnp.cos(blade_angle)[:, None]
    sine = jnp.sin(blade_angle)[:, None]
    factor = jnp.where(
        offset_of[None, :] < 2 * INF,
        jnp.float32(1.0),
        jnp.where(offset_of[None, :] < 3 * INF, cosine, sine),
    )
    return jnp.where(
        sensor_turbine[:, None] == turbine_of[None, :], weights * factor, jnp.float32(0.0)
    )


def split_bf16(x):
    high = x.astype(jnp.bfloat16)
    low = (x - high.astype(jnp.float32)).astype(jnp.bfloat16)
    return high, low


def coupling_matrix(wake_block, upstream, turbine):
    slots = upstream[turbine]
    blocks = jnp.zeros((INF, TURB, INF), jnp.bfloat16)
    for slot_index in range(NUP):
        anchor = slots[slot_index]
        hit = (jnp.arange(TURB) == anchor)[None, :, None]
        blocks = blocks + jnp.where(
            hit, wake_block[turbine, slot_index][:, None, :], jnp.zeros((), jnp.bfloat16)
        )
    return blocks.reshape(INF, TURB * INF)


def dot_f32(a, b, dims):
    return lax.dot_general(a, b, (dims, ((), ())), preferred_element_type=jnp.float32)


def shards(
    covariance,
    self_block,
    wake_block,
    upstream,
    process_noise,
    sensor_turbine,
    azimuth_index,
    sensor_weight,
    sensor_noise,
):
    row_count, col_count = covariance.shape
    row_start = lax.axis_index("row") * row_count
    col_start = lax.axis_index("col") * col_count
    per_row = row_count // SPT
    per_col = max(1, col_count // SPT)
    first_turbine = lax.axis_index("row") * per_row

    cov3 = covariance.reshape(per_row, SPT, col_count)
    inflow_all = lax.all_gather(cov3[:, :INF, :], "row", axis=0, tiled=True)
    inflow_high, inflow_low = split_bf16(inflow_all.reshape(TURB * INF, col_count))
    own_rows = lax.all_gather(self_block, "col", axis=0, tiled=True)
    cov_high, cov_low = split_bf16(cov3)
    blocks = []
    for local in range(per_row):
        turbine = first_turbine + local
        diag_rows = own_rows[local * SPT : (local + 1) * SPT]
        result = dot_f32(diag_rows, cov_high[local], ((1,), (0,))) + dot_f32(
            diag_rows, cov_low[local], ((1,), (0,))
        )
        coupling = coupling_matrix(wake_block, upstream, turbine)
        inflow_sum = dot_f32(coupling, inflow_high, ((1,), (0,))) + dot_f32(
            coupling, inflow_low, ((1,), (0,))
        )
        result = jnp.concatenate([result[:INF] + inflow_sum, result[INF:]], 0)
        blocks.append(result.astype(jnp.bfloat16))
    half_product = jnp.concatenate(blocks, 0)

    if col_count >= SPT:
        half3 = half_product.reshape(row_count, per_col, SPT)
        half_inflow = jnp.transpose(half3[:, :, :INF], (1, 0, 2))
        half_inflow_all = lax.all_gather(half_inflow, "col", axis=0, tiled=True)
        turbine_cols = [half3[:, local, :] for local in range(per_col)]
    else:
        full = lax.all_gather(half_product, "col", axis=1, tiled=True)
        half_inflow_all = jnp.transpose(full.reshape(row_count, TURB, SPT)[:, :, :INF], (1, 0, 2))
        turbine_cols = [lax.dynamic_slice_in_dim(full, (col_start // SPT) * SPT, SPT, 1)]
    target_rows = lax.dynamic_slice_in_dim(own_rows, col_start % row_count, col_count, 0)
    target_rows = broadcast(target_rows, "row", col_start // row_count)
    piece_width = min(col_count, SPT)
    pieces = []
    for local in range(per_col):
        turbine = col_start // SPT + local
        diag_rows = target_rows[local * piece_width : (local + 1) * piece_width]
        result = dot_f32(turbine_cols[local], diag_rows, ((1,), (1,)))
        coupling = coupling_matrix(wake_block, upstream, turbine).reshape(INF, TURB, INF)
        inflow_sum = dot_f32(half_inflow_all, coupling, ((0, 2), (1, 2)))
        inflow_sum = jnp.where(col_start % SPT == 0, inflow_sum, jnp.float32(0.0))
        pieces.append(jnp.concatenate([result[:, :INF] + inflow_sum, result[:, INF:]], 1))
    predicted = jnp.concatenate(pieces, 1)
    row_ids = row_start + jnp.arange(row_count)
    col_ids = col_start + jnp.arange(col_count)
    predicted = predicted + jnp.where(
        row_ids[:, None] == col_ids[None, :], process_noise[None, :], jnp.float32(0.0)
    )

    col_observe = observe_columns(
        sensor_weight, sensor_turbine, azimuth_index, col_start, col_count
    )
    partial_cross = jnp.dot(predicted, col_observe.T, precision=lax.Precision.HIGHEST)
    cross_cov = lax.psum(partial_cross, "col")
    row_observe = observe_columns(
        sensor_weight, sensor_turbine, azimuth_index, row_start, row_count
    )
    partial_innovation = jnp.dot(row_observe, cross_cov, precision=lax.Precision.HIGHEST)
    innovation = lax.psum(partial_innovation, "row") + jnp.diag(sensor_noise)
    symmetric = 0.5 * (innovation + innovation.T)
    lower = jnp.linalg.cholesky(symmetric)
    sensors = symmetric.shape[0]
    lower_inverse = jax.scipy.linalg.solve_triangular(
        lower, jnp.eye(sensors, dtype=jnp.float32), lower=True
    )
    inverse = jnp.dot(lower_inverse.T, lower_inverse, precision=lax.Precision.HIGHEST)
    gain_block = jnp.dot(cross_cov, inverse, precision=lax.Precision.HIGHEST)
    target_cross = lax.dynamic_slice_in_dim(cross_cov, col_start % row_count, col_count, 0)
    target_cross = broadcast(target_cross, "row", col_start // row_count)
    posterior = predicted - jnp.dot(gain_block, target_cross.T, precision=lax.Precision.HIGHEST)
    share = gain_block.shape[1] // lax.axis_size("col")
    gain_share = lax.dynamic_slice_in_dim(gain_block, lax.axis_index("col") * share, share, 1)
    return (posterior, gain_share)


def solution(mesh):
    in_specs = (P("row", "col"), P(("row", "col"), None), P(), P(), P("col"), P(), P(), P(), P())
    out_specs = (P("row", "col"), P("row", "col"))
    return jax.shard_map(shards, mesh=mesh, in_specs=in_specs, out_specs=out_specs, check_vma=False)
```

time: 1210 us -> 690 us (0.57)
  waiting for transfers between devices: 849 us -> 350 us
  matrix products: 141 us -> 112 us
  other arithmetic: 121 us -> 144 us
  between operations: 37.6 us -> 17.8 us
    all_gather x2, waiting for transfers between devices: 682 us -> 173 us  [the longest x1 130 us: shards(): inflow_all = lax.all_gather(cov3[:, :INF, :], 'row', axis=0, tiled=True)]
    psum x0 -> x1, waiting for transfers between devices: none -> 88.4 us  [shards(): innovation = lax.psum(partial_innovation, 'row') + jnp.diag(sensor_noise)]
    psum x2 -> x1, waiting for transfers between devices: 89.8 us -> 20.8 us  [broadcast(): return lax.psum(jnp.where(mine, value, jnp.zeros_like(value)), axis)]
    dot_general x21 -> x22, matrix products: 74.1 us -> 40.9 us  [the longest x20 34.1 us: dot_f32(): lax.dot_general(a, b, (dims, ((), ())), preferred_element_type=jnp.float32)]
    dot_general x1, matrix products: 15.8 us -> 38.5 us  [shards(): jnp.dot(predicted, col_observe.T, precision=lax.Precision.HIGHEST)]
    eq x1 -> x25, other arithmetic: 0.01 us -> 22.5 us  [the longest x24 22.5 us: coupling_matrix(): hit = (jnp.arange(TURB) == anchor)[None, :, None]]
    convert_element_type x0 -> x3, other arithmetic: none -> 21.5 us  [the longest x2 20.7 us: split_bf16(): low = (x - high.astype(jnp.float32)).astype(jnp.bfloat16)]
    gather x4 -> x0, local copies, waits for them, and re-layouts: 15 us -> none  [transition_strip(): coefficient = jnp.take(flat_wake, lookup, axis=0)]
  transfers between devices with their start and end apart: 6 -> 6, of which waited for: 5 -> 5; matrix products, arithmetic and copies ran while one was open for 8% -> 13% of each run, Pallas kernels for 0% -> 0%
where the time goes in v1:
time: 690 us; the launch traced here: 682 us
  waiting for transfers between devices  350 us (51%)
  other arithmetic  144 us (21%)
  matrix products  112 us (16%)
  local copies, waits for them, and re-layouts  58.7 us (9%)
  between operations  17.8 us (3%)
    all_gather x1, waiting for transfers between devices, shards(): inflow_all = lax.all_gather(cov3[:, :INF, :], 'row', axis=0, tiled=True)  130 us
    psum x1, waiting for transfers between devices, shards(): innovation = lax.psum(partial_innovation, 'row') + jnp.diag(sensor_noise)  88.4 us
    psum x1, waiting for transfers between devices, shards(): cross_cov = lax.psum(partial_cross, 'col')  66.4 us
    another operation x11, other arithmetic, shards(): lower = jnp.linalg.cholesky(symmetric)  60.4 us
    all_gather x1, waiting for transfers between devices, shards(): half_inflow_all = lax.all_gather(half_inflow, 'col', axis=0, tiled=True)  43.6 us
    dot_general x1, matrix products, shards(): jnp.dot(predicted, col_observe.T, precision=lax.Precision.HIGHEST)  38.5 us
    dot_general x20, matrix products, dot_f32(): lax.dot_general(a, b, (dims, ((), ())), preferred_element_type=jnp.float32)  34.1 us
    another operation x3, other arithmetic, shards(): jax.scipy.linalg.solve_triangular(lower, jnp.eye(sensors, dtype=jnp.float...  32.7 us
  transfers between devices with their start and end apart: 6, of which 5 were waited for; matrix products, arithmetic and copies ran while one was open for 13% of the time, Pallas kernels for 0%

profile of v1, /device:TPU:0, one launch (start us, length us, event | category | flops | bytes accessed | tf_op | source)
XLA Modules:
  0.0 682.4 jit_solution(16363561873510141729)
XLA Ops:
  8.0 3.1 slice.340
  32.1 11.9 %subtract_convert_fusion.1 = (bf16[4,512,1024]{2,1,0:T(8,128)(2,1)}, bf16[4,512,1024]{2,1,0:T(8,128)(2,1)}) fusion(f32[4,512,1024]{2,1,0:T(8,128)} %bitcast.250), kind=kLoop, calls=%fused_computation.4 | loop fusion | flops 8388608 | bytes 16777216 | tf_op jit(solution)/shard_map/convert_element_type | solution.py:47
  62.0 129.8 %all-gather.6.cloned.1.call-done = f32[16,128,1024]{2,1,0:T(8,128)} async-done(((f32[4,128,1024]{2,1,0:T(8,128)}), f32[16,128,1024]{2,1,0:T(8,128)}) %all-gather.6.cloned.1.call-update) | async-done | bytes 8388624 | tf_op jit(solution)/shard_map/all_gather | solution.py:86
  191.8 8.7 %subtract_convert_fusion = (bf16[16,128,1024]{2,1,0:T(8,128)(2,1)S(1)}, bf16[16,128,1024]{2,1,0:T(8,128)(2,1)S(1)}) fusion(f32[16,128,1024]{2,1,0:T(8,128)} %all-gather.6.cloned.1.call-done), kind=kLoop, calls=%fused_computation.3 | loop fusion | flops 8388608 | bytes 16777216 | tf_op jit(solution)/shard_map/convert_element_type | solution.py:47
  223.4 20.8 %all-reduce.6.cloned.1.call-done = bf16[1024,512]{1,0:T(8,128)(2,1)} async-done(((bf16[1024,512]{1,0:T(8,128)(2,1)}), bf16[1024,512]{1,0:T(8,128)(2,1)}) %all-reduce.6.cloned.1.call-update) | async-done | bytes 1048592 | tf_op jit(solution)/shard_map/psum | solution.py:17
  244.2 3.0 fusion.10
  247.4 3.5 copy-done.5
  256.4 43.6 %all-gather.8.cloned.1.call-done = bf16[16,2048,128]{2,1,0:T(8,128)(2,1)} async-done(((bf16[2,2048,128]{2,1,0:T(8,128)(2,1)}), bf16[16,2048,128]{2,1,0:T(8,128)(2,1)}) %all-gather.8.cloned.1.call-update) | async-done | bytes 8388624 | tf_op jit(solution)/shard_map/all_gather | solution.py:108
  299.9 6.6 fusion.9
  306.6 4.5 fusion.8
  312.1 38.5 %fusion.17 = f32[2048,384]{1,0:T(8,128)} fusion(f32[384,1024]{1,0:T(8,128)S(1)} %bitcast.258, f32[384]{0:T(512)S(1)} %get-tuple-element.103, f32[384]{0:T(512)S(1)} %get-tuple-element.102, s32[1024]{0:T(1024)S(1)} %get-tuple-element.104, s32[384]{0:T(512)S(1)} %copy-done.33, pred[1024]{0:T(1024)(128)(4,1)S(1)} %get-tuple-element.106, ...), kind=kOutput, calls=%fused_computation.36 | convolution fusion | flops 9678225408 | bytes 13134336 | tf_op jit(solution)/shard_map/dot_general | solution.py:136
  353.8 66.4 %all-reduce.8.cloned.1.call-done = f32[2048,384]{1,0:T(8,128)} async-done(((f32[2048,384]{1,0:T(8,128)}), f32[2048,384]{1,0:T(8,128)}) %all-reduce.8.cloned.1.call-update) | async-done | bytes 3145744 | tf_op jit(solution)/shard_map/psum | solution.py:137
  422.8 8.5 %fusion = f32[384,384]{0,1:T(8,128)} fusion(f32[2048,384]{1,0:T(8,128)} %all-reduce.8.cloned.1.call-done, f32[384,2048]{1,0:T(8,128)S(1)} %bitcast.253, f32[384]{0:T(512)S(1)} %get-tuple-element.103, f32[384]{0:T(512)S(1)} %get-tuple-element.102, s32[2048]{0:T(1024)S(1)} %add_select_fusion.1, s32[384]{0:T(512)S(1)} %copy-done.33, ...), kind=kOutput, calls=%fused_computation.6 | convolution fusion | flops 3627810816 | bytes 6898176 | tf_op jit(solution)/shard_map/dot_general | solution.py:141
  432.8 88.4 %all-reduce.10.cloned.1.call-done = (f32[384,384]{0,1:T(8,128)}, f32[1024,384]{1,0:T(8,128)}) async-done(((f32[384,384]{0,1:T(8,128)}, f32[1024,384]{1,0:T(8,128)}), (f32[384,384]{0,1:T(8,128)}, f32[1024,384]{1,0:T(8,128)})) %all-reduce.10.cloned.1.call-update) | async-done | bytes 2162704 | tf_op jit(solution)/shard_map/psum | solution.py:142
  524.0 11.8 %cholesky.76 = f32[128,128]{1,0:T(8,128)S(1)} custom-call(f32[128,128]{1,0:T(8,128)S(1)} %cholesky.189), custom_call_target="Cholesky" | custom-call | tf_op jit(solution)/shard_map/jit(cholesky)/cholesky | solution.py:144
  536.6 9.8 %custom-call.23 = f32[1,128,128]{1,2,0:T(8,128)S(1)} custom-call(f32[1,128,128]{2,1,0:T(8,128)S(1)} %get-tuple-element.71), custom_call_target="InvertDiagBlocksLowerTriangular" | custom-call | tf_op jit(solution)/shard_map/jit(cholesky)/cholesky | solution.py:144
  547.1 11.7 %cholesky.160 = f32[128,128]{1,0:T(8,128)S(1)} custom-call(f32[128,128]{1,0:T(8,128)S(1)} %cholesky.193), custom_call_target="Cholesky" | custom-call | tf_op jit(solution)/shard_map/jit(cholesky)/cholesky | solution.py:144
  560.1 10.4 %custom-call.24 = f32[1,128,128]{1,2,0:T(8,128)} custom-call(f32[1,128,128]{2,1,0:T(8,128)S(1)} %get-tuple-element.69), custom_call_target="InvertDiagBlocksLowerTriangular" | custom-call | tf_op jit(solution)/shard_map/jit(cholesky)/cholesky | solution.py:144
  574.8 11.9 %cholesky.179 = f32[128,128]{1,0:T(8,128)S(1)} custom-call(f32[128,128]{1,0:T(8,128)S(1)} %convolution_subtract_fusion.4), custom_call_target="Cholesky" | custom-call | tf_op jit(solution)/shard_map/jit(cholesky)/cholesky | solution.py:144
  595.3 11.1 %while.1 = (s32[]{:T(128)}, f32[384,384]{0,1:T(8,128)}, s32[3,2]{0,1:T(2,128)S(1)}, f32[3,128,128]{2,1,0:T(8,128)}, s32[]{:T(128)}) while((s32[]{:T(128)}, f32[384,384]{0,1:T(8,128)}, s32[3,2]{0,1:T(2,128)S(1)}, f32[3,128,128]{2,1,0:T(8,128)}, s32[]{:T(128)}) %tuple.95), condition=%wide.while_cond, body=%wide.while_body.sunk | while | flops 2 | bytes 393329 | solution.py:146
  606.4 30.3 %custom-call.25 = f32[3,128,128]{1,2,0:T(8,128)S(1)} custom-call(f32[3,128,128]{2,1,0:T(8,128)} %get-tuple-element.9), custom_call_target="InvertDiagBlocksLowerTriangular" | custom-call | tf_op jit(solution)/shard_map/jit(_solve_triangular)/triangular_solve | solution.py:146
  642.8 5.4 fusion.158
  648.3 16.8 %convolution_subtract_fusion = f32[2048,1024]{0,1:T(8,128)} fusion(f32[2048,384]{0,1:T(8,128)S(1)} %fusion.158, f32[1024,384]{1,0:T(8,128)S(1)} %copy-done.36, f32[1024]{0:T(1024)S(1)} %copy-done.38, s32[1024]{0:T(1024)S(1)} %copy-done.32, s32[2048]{0:T(1024)S(1)} %copy-done.29, f32[2048,384]{0,1:T(8,128)S(1)} %copy-done.12, f32[2048,128]{0,1:T(8,128)S(1)} %copy-done.56, ...), kind=kOutput, calls=%fused_computation.5 | convolution fusion | flops 9678356480 | bytes 21512192 | tf_op jit(solution)/shard_map/dot_general | solution.py:153
  665.9 9.2 %copy.81 = f32[2048,1024]{1,0:T(8,128)} copy(f32[2048,1024]{0,1:T(8,128)} %convolution_subtract_fusion) | data formatting | bytes 16777216
  (253 shorter events, 109.8 us)
Async XLA Ops:
  7.2 36.8 %all-gather.4.cloned.1.call-start = ((), (), s32[]{:S(2)}) async-start(), calls=%async_computation | async-start | bytes 2359296 | tf_op jit(solution)/shard_map/all_gather | solution.py:88
  7.9 183.8 %all-gather.6.cloned.1.call-start = ((), (), s32[]{:S(2)}) async-start(), calls=%async_computation.1 | async-start | bytes 10485760 | tf_op jit(solution)/shard_map/all_gather | solution.py:86
  11.1 233.1 %all-reduce.6.cloned.1.call-start = ((), (), s32[]{:S(2)}) async-start(), calls=%async_computation.2 | async-start | bytes 2097152 | tf_op jit(solution)/shard_map/psum | solution.py:17
  61.7 238.3 %all-gather.8.cloned.1.call-start = ((), (), s32[]{:S(2)}) async-start(), calls=%async_computation.3 | async-start | bytes 9437184 | tf_op jit(solution)/shard_map/all_gather | solution.py:108
  191.8 8.8 %copy-start.24 = (bf16[128,128]{1,0:T(8,128)(2,1)S(1)}, bf16[128,128]{1,0:T(8,128)(2,1)}, u32[]{:S(2)}) copy-start(bf16[128,128]{1,0:T(8,128)(2,1)} %get-tuple-element.54) | copy-start | bytes 98308
  191.8 8.8 %copy-start.25 = (bf16[128,128]{1,0:T(8,128)(2,1)S(1)}, bf16[128,128]{1,0:T(8,128)(2,1)}, u32[]{:S(2)}) copy-start(bf16[128,128]{1,0:T(8,128)(2,1)} %get-tuple-element.55) | copy-start | bytes 98308
  191.8 8.8 %copy-start.26 = (bf16[128,128]{1,0:T(8,128)(2,1)S(1)}, bf16[128,128]{1,0:T(8,128)(2,1)}, u32[]{:S(2)}) copy-start(bf16[128,128]{1,0:T(8,128)(2,1)} %get-tuple-element.56) | copy-start | bytes 98308
  191.8 8.8 %copy-start.27 = (bf16[128,128]{1,0:T(8,128)(2,1)S(1)}, bf16[128,128]{1,0:T(8,128)(2,1)}, u32[]{:S(2)}) copy-start(bf16[128,128]{1,0:T(8,128)(2,1)} %get-tuple-element.57) | copy-start | bytes 98308
  214.3 8.9 %copy-start.33 = (s32[384]{0:T(512)S(1)}, s32[384]{0:T(512)}, u32[]{:S(2)}) copy-start(s32[384]{0:T(512)} %param.14) | copy-start | bytes 4612
  214.3 8.9 %copy-start.34 = (s32[16]{0:T(128)S(1)}, s32[16]{0:T(128)}, u32[]{:S(2)}) copy-start(s32[16]{0:T(128)} %param.15) | copy-start | bytes 196
  215.5 204.7 %all-reduce.8.cloned.1.call-start = ((), (), s32[]{:S(2)}) async-start(), calls=%async_computation.4 | async-start | bytes 6291456 | tf_op jit(solution)/shard_map/psum | solution.py:137
  223.2 87.9 %copy-start.31 = (s32[1024]{0:T(1024)}, s32[1024]{0:T(1024)S(1)}, u32[]{:S(2)}) copy-start(s32[1024]{0:T(1024)S(1)} %get-tuple-element.105) | copy-start | bytes 12292
  223.3 87.9 %copy-start.28 = (s32[2048]{0:T(1024)}, s32[2048]{0:T(1024)S(1)}, u32[]{:S(2)}) copy-start(s32[2048]{0:T(1024)S(1)} %iota_add_fusion) | copy-start | bytes 24580
  251.2 59.9 %copy-start.11 = (f32[2048,384]{0,1:T(8,128)}, f32[2048,384]{0,1:T(8,128)S(1)}, u32[]{:S(2)}) copy-start(f32[2048,384]{0,1:T(8,128)S(1)} %slice.365) | copy-start | bytes 9437188
  350.6 170.6 %all-reduce.10.cloned.1.call-start = ((), (), s32[]{:S(2)}) async-start(), calls=%async_computation.5 | async-start | bytes 4325376 | tf_op jit(solution)/shard_map/psum | solution.py:142
  422.8 98.4 %copy-start.30 = (f32[384]{0:T(512)S(1)}, f32[384]{0:T(512)}, u32[]{:S(2)}) copy-start(f32[384]{0:T(512)} %param.17) | copy-start | bytes 4612
  524.0 46.6 %copy-start.20 = (f32[384,384]{1,0:T(8,128)}, f32[384,384]{1,0:T(8,128)S(1)}, u32[]{:S(2)}) copy-start(f32[384,384]{1,0:T(8,128)S(1)} %fusion.56) | copy-start | bytes 1769476
  570.6 72.2 %copy-start.7 = (f32[2048,384]{1,0:T(8,128)S(1)}, f32[2048,384]{1,0:T(8,128)}, u32[]{:S(2)}) copy-start(f32[2048,384]{1,0:T(8,128)} %all-reduce.8.cloned.1.call-done) | copy-start | bytes 9437188
  637.0 11.1 %copy-start.56 = (f32[2048,128]{0,1:T(8,128)S(1)}, f32[2048,128]{0,1:T(8,128)}, u32[]{:S(2)}) copy-start(f32[2048,128]{0,1:T(8,128)} %copy-done.55) | copy-start | bytes 3145732
  639.0 9.2 %copy-start.54 = (f32[2048,128]{0,1:T(8,128)S(1)}, f32[2048,128]{0,1:T(8,128)}, u32[]{:S(2)}) copy-start(f32[2048,128]{0,1:T(8,128)} %copy-done.53) | copy-start | bytes 3145732
  640.9 7.3 %copy-start.12 = (f32[2048,384]{0,1:T(8,128)S(1)}, f32[2048,384]{0,1:T(8,128)}, u32[]{:S(2)}) copy-start(f32[2048,384]{0,1:T(8,128)} %copy-done.11) | copy-start | bytes 9437188
  640.9 7.3 %copy-start.14 = (f32[2048,384]{0,1:T(8,128)S(1)}, f32[2048,384]{0,1:T(8,128)}, u32[]{:S(2)}) copy-start(f32[2048,384]{0,1:T(8,128)} %slice.361) | copy-start | bytes 9437188
  640.9 7.3 %copy-start.29 = (s32[2048]{0:T(1024)S(1)}, s32[2048]{0:T(1024)}, u32[]{:S(2)}) copy-start(s32[2048]{0:T(1024)} %copy-done.28) | copy-start | bytes 24580
  640.9 7.3 %copy-start.32 = (s32[1024]{0:T(1024)S(1)}, s32[1024]{0:T(1024)}, u32[]{:S(2)}) copy-start(s32[1024]{0:T(1024)} %copy-done.31) | copy-start | bytes 12292
  (39 other events, 118.0 us)
Sparse Core Ops, SparseCore 0:
  9.9 30.5 all-gather.3
  42.1 149.6 all-gather.5
  194.1 50.0 all-reduce.5
  246.1 53.7 all-gather.7
  350.7 69.4 all-reduce.7
  431.5 89.6 all-reduce.9

commit v2 on v1

--- a/solution.py
+++ b/solution.py
@@ -43,9 +43,21 @@
 
 
 def split_bf16(x):
-    high = x.astype(jnp.bfloat16)
-    low = (x - high.astype(jnp.float32)).astype(jnp.bfloat16)
-    return high, low
+    high = lax.reduce_precision(x, exponent_bits=8, mantissa_bits=7)
+    return high.astype(jnp.bfloat16), (x - high).astype(jnp.bfloat16)
+
+
+def column_rows(local_rows, col_count):
+    nrow = lax.axis_size("row")
+    ncol = lax.axis_size("col")
+    devices = nrow * ncol
+    pieces = []
+    for step in range(nrow):
+        perm = [(d, ((d % nrow + step) % nrow) * ncol + d // nrow) for d in range(devices)]
+        pieces.append(lax.ppermute(local_rows, ("row", "col"), perm))
+    stacked = jnp.stack(pieces, 0)
+    order = (lax.axis_index("row") - jnp.arange(nrow)) % nrow
+    return jnp.take(stacked, order, axis=0).reshape((col_count,) + local_rows.shape[1:])
 
 
 def coupling_matrix(wake_block, upstream, turbine):
@@ -83,8 +95,9 @@
     first_turbine = lax.axis_index("row") * per_row
 
     cov3 = covariance.reshape(per_row, SPT, col_count)
-    inflow_all = lax.all_gather(cov3[:, :INF, :], "row", axis=0, tiled=True)
-    inflow_high, inflow_low = split_bf16(inflow_all.reshape(TURB * INF, col_count))
+    inflow_part = cov3[:, :INF, :].astype(jnp.bfloat16)
+    inflow_all = lax.all_gather(inflow_part, "row", axis=0, tiled=True)
+    inflow_all = inflow_all.reshape(TURB * INF, col_count)
     own_rows = lax.all_gather(self_block, "col", axis=0, tiled=True)
     cov_high, cov_low = split_bf16(cov3)
     blocks = []
@@ -95,9 +108,7 @@
             diag_rows, cov_low[local], ((1,), (0,))
         )
         coupling = coupling_matrix(wake_block, upstream, turbine)
-        inflow_sum = dot_f32(coupling, inflow_high, ((1,), (0,))) + dot_f32(
-            coupling, inflow_low, ((1,), (0,))
-        )
+        inflow_sum = dot_f32(coupling, inflow_all, ((1,), (0,)))
         result = jnp.concatenate([result[:INF] + inflow_sum, result[INF:]], 0)
         blocks.append(result.astype(jnp.bfloat16))
     half_product = jnp.concatenate(blocks, 0)
@@ -111,8 +122,7 @@
         full = lax.all_gather(half_product, "col", axis=1, tiled=True)
         half_inflow_all = jnp.transpose(full.reshape(row_count, TURB, SPT)[:, :, :INF], (1, 0, 2))
         turbine_cols = [lax.dynamic_slice_in_dim(full, (col_start // SPT) * SPT, SPT, 1)]
-    target_rows = lax.dynamic_slice_in_dim(own_rows, col_start % row_count, col_count, 0)
-    target_rows = broadcast(target_rows, "row", col_start // row_count)
+    target_rows = column_rows(self_block, col_count)
     piece_width = min(col_count, SPT)
     pieces = []
     for local in range(per_col):
@@ -148,8 +158,9 @@
     )
     inverse = jnp.dot(lower_inverse.T, lower_inverse, precision=lax.Precision.HIGHEST)
     gain_block = jnp.dot(cross_cov, inverse, precision=lax.Precision.HIGHEST)
-    target_cross = lax.dynamic_slice_in_dim(cross_cov, col_start % row_count, col_count, 0)
-    target_cross = broadcast(target_cross, "row", col_start // row_count)
+    piece = self_block.shape[0]
+    own_piece = lax.dynamic_slice_in_dim(cross_cov, lax.axis_index("col") * piece, piece, 0)
+    target_cross = column_rows(own_piece, col_count)
     posterior = predicted - jnp.dot(gain_block, target_cross.T, precision=lax.Precision.HIGHEST)
     share = gain_block.shape[1] // lax.axis_size("col")
     gain_share = lax.dynamic_slice_in_dim(gain_block, lax.axis_index("col") * share, share, 1)

time: 690 us -> 544 us (0.79)
  waiting for transfers between devices: 350 us -> 205 us
  starting transfers between devices: 0.5 us -> 24.7 us
  other arithmetic: 144 us -> 128 us
  matrix products: 112 us -> 101 us
    all_gather x1, waiting for transfers between devices: 130 us -> 67.7 us  [shards(): inflow_all = lax.all_gather(inflow_part, 'row', axis=0, tiled=True)]
    psum x1, waiting for transfers between devices: 88.4 us -> 29 us  [shards(): innovation = lax.psum(partial_innovation, 'row') + jnp.diag(sensor_noise)]
    ppermute x0 -> x8, starting transfers between devices: none -> 24.5 us  [column_rows(): pieces.append(lax.ppermute(local_rows, ('row', 'col'), perm))]
    psum x1 -> x0, waiting for transfers between devices: 20.8 us -> none  [broadcast(): return lax.psum(jnp.where(mine, value, jnp.zeros_like(value)), axis)]
    all_gather x1, waiting for transfers between devices: 43.6 us -> 29.6 us  [shards(): half_inflow_all = lax.all_gather(half_inflow, 'col', axis=0, tiled=True)]
    ppermute x0 -> x8, waiting for transfers between devices: none -> 13 us  [column_rows(): pieces.append(lax.ppermute(local_rows, ('row', 'col'), perm))]
    convert_element_type x2 -> x1, other arithmetic: 20.7 us -> 8.68 us  [split_bf16(): return (high.astype(jnp.bfloat16), (x - high).astype(jnp.bfloat16))]
    dot_general x1, matrix products: 38.5 us -> 29.1 us  [shards(): jnp.dot(predicted, col_observe.T, precision=lax.Precision.HIGHEST)]
  transfers between devices with their start and end apart: 6 -> 13, of which waited for: 5 -> 7; matrix products, arithmetic and copies ran while one was open for 13% -> 14% of each run, Pallas kernels for 0% -> 0%
where the time goes in v2:
time: 544 us; the launch traced here: 534 us
  waiting for transfers between devices  205 us (38%)
  other arithmetic  128 us (24%)
  matrix products  101 us (19%)
  local copies, waits for them, and re-layouts  59.1 us (11%)
  starting transfers between devices  24.7 us (5%)
  between operations  17.2 us (3%)
    all_gather x1, waiting for transfers between devices, shards(): inflow_all = lax.all_gather(inflow_part, 'row', axis=0, tiled=True)  67.7 us
    psum x1, waiting for transfers between devices, shards(): cross_cov = lax.psum(partial_cross, 'col')  65.2 us
    another operation x11, other arithmetic, shards(): lower = jnp.linalg.cholesky(symmetric)  57.2 us
    another operation x3, other arithmetic, shards(): jax.scipy.linalg.solve_triangular(lower, jnp.eye(sensors, dtype=jnp.float...  31.2 us
    dot_general x16, matrix products, dot_f32(): lax.dot_general(a, b, (dims, ((), ())), preferred_element_type=jnp.float32)  30.3 us
    all_gather x1, waiting for transfers between devices, shards(): half_inflow_all = lax.all_gather(half_inflow, 'col', axis=0, tiled=True)  29.6 us
    dot_general x1, matrix products, shards(): jnp.dot(predicted, col_observe.T, precision=lax.Precision.HIGHEST)  29.1 us
    psum x1, waiting for transfers between devices, shards(): innovation = lax.psum(partial_innovation, 'row') + jnp.diag(sensor_noise)  29 us
  transfers between devices with their start and end apart: 13, of which 7 were waited for; matrix products, arithmetic and copies ran while one was open for 14% of the time, Pallas kernels for 0%

profile of v2, /device:TPU:0, one launch (start us, length us, event | category | flops | bytes accessed | tf_op | source)
XLA Modules:
  0.0 534.4 jit_solution(14048635772002735833)
XLA Ops:
  31.8 8.7 %fusion = (bf16[4,512,1024]{2,1,0:T(8,128)(2,1)}, bf16[4,512,1024]{2,1,0:T(8,128)(2,1)}) fusion(f32[4,512,1024]{2,1,0:T(8,128)} %bitcast.247), kind=kLoop, calls=%fused_computation.6 | loop fusion | flops 8388608 | bytes 16777216 | tf_op jit(solution)/shard_map/convert_element_type | solution.py:47
  55.2 67.7 %all-gather.6.cloned.1.call-done = bf16[16,128,1024]{2,1,0:T(8,128)(2,1)} async-done(((bf16[4,128,1024]{2,1,0:T(8,128)(2,1)}), bf16[16,128,1024]{2,1,0:T(8,128)(2,1)}) %all-gather.6.cloned.1.call-update) | async-done | bytes 4194320 | tf_op jit(solution)/shard_map/all_gather | solution.py:99
  122.9 3.3 fusion.34
  136.0 6.1 %collective-permute-start.1 = (bf16[256,512]{1,0:T(8,128)(2,1)S(1)}, bf16[256,512]{1,0:T(8,128)(2,1)S(1)}, u32[]{:S(2)}, u32[]{:S(2)}) collective-permute-start(bf16[256,512]{1,0:T(8,128)(2,1)S(1)} %copy-done.23), channel_id=1, source_target_pairs={{0,8},{1,16},{2,24},{3,0},{4,9},{5,17},{6,25},{7,1},{8,10},{9,18},... | collective-permute-start | bytes 786440 | tf_op jit(solution)/shard_map/ppermute | solution.py:57
  169.4 29.6 %all-gather.8.cloned.1.call-done = bf16[16,2048,128]{2,1,0:T(8,128)(2,1)} async-done(((bf16[2,2048,128]{2,1,0:T(8,128)(2,1)}), bf16[16,2048,128]{2,1,0:T(8,128)(2,1)}) %all-gather.8.cloned.1.call-update) | async-done | bytes 8388624 | tf_op jit(solution)/shard_map/all_gather | solution.py:119
  199.0 6.6 %fusion.10 = f32[2048,128]{0,1:T(8,128)S(1)} fusion(bf16[16,2048,128]{2,1,0:T(8,128)(2,1)} %all-gather.8.cloned.1.call-done, f32[2048,512]{0,1:T(8,128)} %copy-done.1, pred[16]{0:T(512)(128)(4,1)S(1)} %iota_compare_fusion.9, pred[16]{0:T(512)(128)(4,1)S(1)} %iota_compare_fusion.10, pred[16]{0:T(512)(128)(4,1)S(1)} %iota_compare_fusion.11, ...), kind=kOutput, calls=%fused_computation.20 | convolution fusion | flops 1076101120 | bytes 10616897 | tf_op jit(solution)/shard_map/dot_general | solution.py:76
  205.6 4.5 fusion.9
  211.1 29.1 %fusion.18 = f32[2048,384]{1,0:T(8,128)} fusion(f32[384,1024]{1,0:T(8,128)S(1)} %bitcast.256, f32[384]{0:T(512)S(1)} %get-tuple-element.101, f32[384]{0:T(512)S(1)} %get-tuple-element.100, s32[1024]{0:T(1024)S(1)} %get-tuple-element.102, s32[384]{0:T(512)S(1)} %copy-done.31, pred[1024]{0:T(1024)(128)(4,1)S(1)} %get-tuple-element.104, ...), kind=kOutput, calls=%fused_computation.41 | convolution fusion | flops 9678225408 | bytes 13134336 | tf_op jit(solution)/shard_map/dot_general | solution.py:146
  244.6 65.2 %all-reduce.4.cloned.1.call-done = f32[2048,384]{1,0:T(8,128)} async-done(((f32[2048,384]{1,0:T(8,128)}), f32[2048,384]{1,0:T(8,128)}) %all-reduce.4.cloned.1.call-update) | async-done | bytes 3145744 | tf_op jit(solution)/shard_map/psum | solution.py:147
  313.2 5.1 collective-permute-start.5
  320.0 4.4 collective-permute-start.7
  324.4 8.6 %fusion.1 = f32[384,384]{0,1:T(8,128)} fusion(f32[2048,384]{1,0:T(8,128)} %all-reduce.4.cloned.1.call-done, f32[384,2048]{1,0:T(8,128)S(1)} %bitcast.249, f32[384]{0:T(512)} %copy-done.30, f32[384]{0:T(512)} %copy-done.29, s32[2048]{0:T(1024)S(1)} %add_select_fusion.1, s32[384]{0:T(512)} %param.14, pred[2048]{0:T(1024)(128)(4,1)} %get-tuple-element.106, ...), kind=kOutput, calls=%fused_computation.9 | convolution fusion | flops 3627810816 | bytes 6898176 | tf_op jit(solution)/shard_map/dot_general | solution.py:151
  336.7 8.2 %collective-permute-done.7 = f32[256,384]{1,0:T(8,128)} collective-permute-done((f32[256,384]{1,0:T(8,128)}, f32[256,384]{1,0:T(8,128)}, u32[]{:S(2)}, u32[]{:S(2)}) %collective-permute-start.7) | collective-permute-done | bytes 393248 | tf_op jit(solution)/shard_map/ppermute | solution.py:57
  348.5 29.0 %all-reduce.6.cloned.1.call-done = f32[384,384]{0,1:T(8,128)} async-done(((f32[384,384]{0,1:T(8,128)}), f32[384,384]{0,1:T(8,128)}) %all-reduce.6.cloned.1.call-update) | async-done | bytes 589840 | tf_op jit(solution)/shard_map/psum | solution.py:152
  380.3 11.7 %cholesky.76 = f32[128,128]{1,0:T(8,128)S(1)} custom-call(f32[128,128]{1,0:T(8,128)S(1)} %cholesky.189), custom_call_target="Cholesky" | custom-call | tf_op jit(solution)/shard_map/jit(cholesky)/cholesky | solution.py:154
  392.1 10.2 %custom-call.23 = f32[1,128,128]{1,2,0:T(8,128)S(1)} custom-call(f32[1,128,128]{2,1,0:T(8,128)S(1)} %get-tuple-element.69), custom_call_target="InvertDiagBlocksLowerTriangular" | custom-call | tf_op jit(solution)/shard_map/jit(cholesky)/cholesky | solution.py:154
  402.8 11.7 %cholesky.160 = f32[128,128]{1,0:T(8,128)S(1)} custom-call(f32[128,128]{1,0:T(8,128)S(1)} %cholesky.193), custom_call_target="Cholesky" | custom-call | tf_op jit(solution)/shard_map/jit(cholesky)/cholesky | solution.py:154
  414.9 9.8 %custom-call.24 = f32[1,128,128]{1,2,0:T(8,128)S(1)} custom-call(f32[1,128,128]{2,1,0:T(8,128)S(1)} %get-tuple-element.67), custom_call_target="InvertDiagBlocksLowerTriangular" | custom-call | tf_op jit(solution)/shard_map/jit(cholesky)/cholesky | solution.py:154
  425.5 11.7 %cholesky.179 = f32[128,128]{1,0:T(8,128)S(1)} custom-call(f32[128,128]{1,0:T(8,128)S(1)} %convolution_subtract_fusion.4), custom_call_target="Cholesky" | custom-call | tf_op jit(solution)/shard_map/jit(cholesky)/cholesky | solution.py:154
  442.1 11.1 %while.1 = (s32[]{:T(128)}, f32[384,384]{0,1:T(8,128)}, s32[3,2]{0,1:T(2,128)S(1)}, f32[3,128,128]{2,1,0:T(8,128)}, s32[]{:T(128)}) while((s32[]{:T(128)}, f32[384,384]{0,1:T(8,128)}, s32[3,2]{0,1:T(2,128)S(1)}, f32[3,128,128]{2,1,0:T(8,128)}, s32[]{:T(128)}) %tuple.95), condition=%wide.while_cond, body=%wide.while_body.sunk | while | flops 2 | bytes 393829 | solution.py:156
  453.2 30.3 %custom-call.25 = f32[3,128,128]{1,2,0:T(8,128)S(1)} custom-call(f32[3,128,128]{2,1,0:T(8,128)} %get-tuple-element.9), custom_call_target="InvertDiagBlocksLowerTriangular" | custom-call | tf_op jit(solution)/shard_map/jit(_solve_triangular)/triangular_solve | solution.py:156
  490.1 5.4 %fusion.217 = f32[2048,384]{0,1:T(8,128)S(1)} fusion(f32[2048,384]{1,0:T(8,128)S(1)} %copy-done.7, f32[384,384]{1,0:T(8,128)S(1)} %fusion.47), kind=kOutput, calls=%fused_computation.379 | convolution fusion | flops 3623878656 | bytes 6881280 | tf_op jit(solution)/shard_map/dot_general | solution.py:160
  497.1 19.5 %convolution_subtract_fusion = f32[2048,1024]{0,1:T(8,128)} fusion(f32[2048,384]{0,1:T(8,128)S(1)} %fusion.217, f32[1024,384]{1,0:T(8,128)S(1)} %copy-done.21, f32[1024]{0:T(1024)S(1)} %copy-done.37, s32[1024]{0:T(1024)S(1)} %copy-done.28, s32[2048]{0:T(1024)S(1)} %iota_add_fusion, f32[2048,384]{0,1:T(8,128)S(1)} %copy-done.15, f32[2048,128]{0,1:T(8,128)} %copy-done.49, ...), kind=kOutput, calls=%fused_computation.8 | convolution fusion | flops 9678356480 | bytes 21512192 | tf_op jit(solution)/shard_map/dot_general | solution.py:164
  516.6 9.2 %copy.81 = f32[2048,1024]{1,0:T(8,128)} copy(f32[2048,1024]{0,1:T(8,128)} %convolution_subtract_fusion) | data formatting | bytes 16777216
  (258 shorter events, 121.6 us)
Async XLA Ops:
  7.2 33.4 %all-gather.4.cloned.1.call-start = ((), (), s32[]{:S(2)}) async-start(), calls=%async_computation | async-start | bytes 2359296 | tf_op jit(solution)/shard_map/all_gather | solution.py:101
  7.9 115.0 %all-gather.6.cloned.1.call-start = ((), (), s32[]{:S(2)}) async-start(), calls=%async_computation.1 | async-start | bytes 5242880 | tf_op jit(solution)/shard_map/all_gather | solution.py:99
  10.7 188.2 %all-gather.8.cloned.1.call-start = ((), (), s32[]{:S(2)}) async-start(), calls=%async_computation.2 | async-start | bytes 9437184 | tf_op jit(solution)/shard_map/all_gather | solution.py:119
  131.9 20.4 %copy-start.31 = (s32[384]{0:T(512)S(1)}, s32[384]{0:T(512)}, u32[]{:S(2)}) copy-start(s32[384]{0:T(512)} %param.14) | copy-start | bytes 4612
  131.9 20.4 %copy-start.33 = (s32[16]{0:T(128)S(1)}, s32[16]{0:T(128)}, u32[]{:S(2)}) copy-start(s32[16]{0:T(128)} %param.15) | copy-start | bytes 196
  131.9 21.1 %copy-start.19 = (f32[384,512]{1,0:T(8,128)S(1)}, f32[384,512]{1,0:T(8,128)}, u32[]{:S(2)}) copy-start(f32[384,512]{1,0:T(8,128)} %param.16) | copy-start | bytes 2359300
  135.2 174.6 %all-reduce.4.cloned.1.call-start = ((), (), s32[]{:S(2)}) async-start(), calls=%async_computation.3 | async-start | bytes 6291456 | tf_op jit(solution)/shard_map/psum | solution.py:147
  135.3 19.8 %collective-permute-start = (bf16[256,512]{1,0:T(8,128)(2,1)S(1)}, bf16[256,512]{1,0:T(8,128)(2,1)S(1)}, u32[]{:S(2)}, u32[]{:S(2)}) collective-permute-start(bf16[256,512]{1,0:T(8,128)(2,1)S(1)} %copy-done.23), channel_id=1, source_target_pairs={{0,0},{1,8},{2,16},{3,24},{4,1},{5,9},{6,17},{7,25},{8,2},{9,10},{... | collective-permute-start | bytes 786440 | tf_op jit(solution)/shard_map/ppermute | solution.py:57
  136.0 19.2 %collective-permute-start.1 = (bf16[256,512]{1,0:T(8,128)(2,1)S(1)}, bf16[256,512]{1,0:T(8,128)(2,1)S(1)}, u32[]{:S(2)}, u32[]{:S(2)}) collective-permute-start(bf16[256,512]{1,0:T(8,128)(2,1)S(1)} %copy-done.23), channel_id=1, source_target_pairs={{0,8},{1,16},{2,24},{3,0},{4,9},{5,17},{6,25},{7,1},{8,10},{9,18},... | collective-permute-start | bytes 786440 | tf_op jit(solution)/shard_map/ppermute | solution.py:57
  142.1 15.8 %collective-permute-start.2 = (bf16[256,512]{1,0:T(8,128)(2,1)S(1)}, bf16[256,512]{1,0:T(8,128)(2,1)S(1)}, u32[]{:S(2)}, u32[]{:S(2)}) collective-permute-start(bf16[256,512]{1,0:T(8,128)(2,1)S(1)} %copy-done.23), channel_id=1, source_target_pairs={{0,16},{1,24},{2,0},{3,8},{4,17},{5,25},{6,1},{7,9},{8,18},{9,26},... | collective-permute-start | bytes 786440 | tf_op jit(solution)/shard_map/ppermute | solution.py:57
  143.9 14.0 %collective-permute-start.3 = (bf16[256,512]{1,0:T(8,128)(2,1)S(1)}, bf16[256,512]{1,0:T(8,128)(2,1)S(1)}, u32[]{:S(2)}, u32[]{:S(2)}) collective-permute-start(bf16[256,512]{1,0:T(8,128)(2,1)S(1)} %copy-done.23), channel_id=1, source_target_pairs={{0,24},{1,0},{2,8},{3,16},{4,25},{5,1},{6,9},{7,17},{8,26},{9,2},{... | collective-permute-start | bytes 786440 | tf_op jit(solution)/shard_map/ppermute | solution.py:57
  147.0 11.6 %copy-start.32 = (pred[4]{0:T(512)(128)(4,1)}, pred[4]{0:T(512)(128)(4,1)S(1)}, u32[]{:S(2)}) copy-start(pred[4]{0:T(512)(128)(4,1)S(1)} %compare_and_fusion) | copy-start | bytes 16
  152.3 57.8 %copy-start.27 = (s32[1024]{0:T(1024)}, s32[1024]{0:T(1024)S(1)}, u32[]{:S(2)}) copy-start(s32[1024]{0:T(1024)S(1)} %get-tuple-element.103) | copy-start | bytes 12292
  155.1 55.0 %copy-start.29 = (f32[384]{0:T(512)}, f32[384]{0:T(512)S(1)}, u32[]{:S(2)}) copy-start(f32[384]{0:T(512)S(1)} %get-tuple-element.100) | copy-start | bytes 4612
  155.1 55.0 %copy-start.30 = (f32[384]{0:T(512)}, f32[384]{0:T(512)S(1)}, u32[]{:S(2)}) copy-start(f32[384]{0:T(512)S(1)} %get-tuple-element.101) | copy-start | bytes 4612
  164.2 45.9 %copy-start.12 = (f32[2048,384]{0,1:T(8,128)}, f32[2048,384]{0,1:T(8,128)S(1)}, u32[]{:S(2)}) copy-start(f32[2048,384]{0,1:T(8,128)S(1)} %slice.374) | copy-start | bytes 9437188
  240.2 137.3 %all-reduce.6.cloned.1.call-start = ((), (), s32[]{:S(2)}) async-start(), calls=%async_computation.4 | async-start | bytes 1179648 | tf_op jit(solution)/shard_map/psum | solution.py:152
  311.6 23.0 %collective-permute-start.4 = (f32[256,384]{1,0:T(8,128)}, f32[256,384]{1,0:T(8,128)S(1)}, u32[]{:S(2)}, u32[]{:S(2)}) collective-permute-start(f32[256,384]{1,0:T(8,128)} %constant_dynamic-slice_fusion.2), channel_id=1, source_target_pairs={{0,0},{1,8},{2,16},{3,24},{4,1},{5,9},{6,17},{7,25},{8,2},{9,10},{... | collective-permute-start | bytes 1179656 | tf_op jit(solution)/shard_map/ppermute | solution.py:57
  313.2 21.4 %collective-permute-start.5 = (f32[256,384]{1,0:T(8,128)}, f32[256,384]{1,0:T(8,128)}, u32[]{:S(2)}, u32[]{:S(2)}) collective-permute-start(f32[256,384]{1,0:T(8,128)} %constant_dynamic-slice_fusion.2), channel_id=1, source_target_pairs={{0,8},{1,16},{2,24},{3,0},{4,9},{5,17},{6,25},{7,1},{8,10},{9,18},... | collective-permute-start | bytes 1179656 | tf_op jit(solution)/shard_map/ppermute | solution.py:57
  318.3 18.3 %collective-permute-start.6 = (f32[256,384]{1,0:T(8,128)}, f32[256,384]{1,0:T(8,128)}, u32[]{:S(2)}, u32[]{:S(2)}) collective-permute-start(f32[256,384]{1,0:T(8,128)} %constant_dynamic-slice_fusion.2), channel_id=1, source_target_pairs={{0,16},{1,24},{2,0},{3,8},{4,17},{5,25},{6,1},{7,9},{8,18},{9,26},... | collective-permute-start | bytes 1179656 | tf_op jit(solution)/shard_map/ppermute | solution.py:57
  320.0 24.8 %collective-permute-start.7 = (f32[256,384]{1,0:T(8,128)}, f32[256,384]{1,0:T(8,128)}, u32[]{:S(2)}, u32[]{:S(2)}) collective-permute-start(f32[256,384]{1,0:T(8,128)} %constant_dynamic-slice_fusion.2), channel_id=1, source_target_pairs={{0,24},{1,0},{2,8},{3,16},{4,25},{5,1},{6,9},{7,17},{8,26},{9,2},{... | collective-permute-start | bytes 1179656 | tf_op jit(solution)/shard_map/ppermute | solution.py:57
  346.2 31.3 %copy-start.25 = (f32[384]{0:T(512)S(1)}, f32[384]{0:T(512)}, u32[]{:S(2)}) copy-start(f32[384]{0:T(512)} %param.17) | copy-start | bytes 4612
  442.1 47.9 %copy-start.7 = (f32[2048,384]{1,0:T(8,128)S(1)}, f32[2048,384]{1,0:T(8,128)}, u32[]{:S(2)}) copy-start(f32[2048,384]{1,0:T(8,128)} %all-reduce.4.cloned.1.call-done) | copy-start | bytes 9437188
  488.6 8.5 %copy-start.21 = (f32[1024,384]{1,0:T(8,128)S(1)}, f32[1024,384]{1,0:T(8,128)}, u32[]{:S(2)}) copy-start(f32[1024,384]{1,0:T(8,128)} %bitcast_select_fusion) | copy-start | bytes 4718596
  (39 other events, 135.0 us)
Sparse Core Ops, SparseCore 0:
  9.9 30.5 all-gather.3
  42.1 80.7 all-gather.5
  135.3 63.5 all-gather.7
  240.4 69.4 all-reduce.3
  333.1 44.3 all-reduce.5

commit v3 on v2

--- a/solution.py
+++ b/solution.py
@@ -40,6 +40,19 @@
     return jnp.where(
         sensor_turbine[:, None] == turbine_of[None, :], weights * factor, jnp.float32(0.0)
     )
+
+
+def gather_col(local_rows):
+    ncol = lax.axis_size("col")
+    if ncol > 8:
+        return lax.all_gather(local_rows, "col", axis=0, tiled=True)
+    pieces = [local_rows]
+    for step in range(1, ncol):
+        perm = [(c, (c + step) % ncol) for c in range(ncol)]
+        pieces.append(lax.ppermute(local_rows, "col", perm))
+    stacked = jnp.stack(pieces, 0)
+    order = (lax.axis_index("col") - jnp.arange(ncol)) % ncol
+    return jnp.take(stacked, order, axis=0).reshape((-1,) + local_rows.shape[1:])
 
 
 def split_bf16(x):
@@ -98,7 +111,7 @@
     inflow_part = cov3[:, :INF, :].astype(jnp.bfloat16)
     inflow_all = lax.all_gather(inflow_part, "row", axis=0, tiled=True)
     inflow_all = inflow_all.reshape(TURB * INF, col_count)
-    own_rows = lax.all_gather(self_block, "col", axis=0, tiled=True)
+    own_rows = gather_col(self_block)
     cov_high, cov_low = split_bf16(cov3)
     blocks = []
     for local in range(per_row):
@@ -144,12 +157,13 @@
         sensor_weight, sensor_turbine, azimuth_index, col_start, col_count
     )
     partial_cross = jnp.dot(predicted, col_observe.T, precision=lax.Precision.HIGHEST)
-    cross_cov = lax.psum(partial_cross, "col")
     row_observe = observe_columns(
         sensor_weight, sensor_turbine, azimuth_index, row_start, row_count
     )
-    partial_innovation = jnp.dot(row_observe, cross_cov, precision=lax.Precision.HIGHEST)
-    innovation = lax.psum(partial_innovation, "row") + jnp.diag(sensor_noise)
+    partial_innovation = jnp.dot(row_observe, partial_cross, precision=lax.Precision.HIGHEST)
+    innovation = lax.psum(partial_innovation, ("row", "col")) + jnp.diag(sensor_noise)
+    partial_cross, innovation = lax.optimization_barrier((partial_cross, innovation))
+    cross_cov = lax.psum(partial_cross, "col")
     symmetric = 0.5 * (innovation + innovation.T)
     lower = jnp.linalg.cholesky(symmetric)
     sensors = symmetric.shape[0]

time: 544 us -> 572 us (1.051)
  the two profiles are of different devices: /device:TPU:0 before, /device:TPU:27 now
where the time goes in v3:
time: 572 us; the launch traced here: 563 us
  waiting for transfers between devices  238 us (42%)
  other arithmetic  121 us (21%)
  matrix products  95.4 us (17%)
  local copies, waits for them, and re-layouts  61.1 us (11%)
  starting transfers between devices  29.5 us (5%)
  between operations  17.2 us (3%)
    psum x1, waiting for transfers between devices, shards(): lax.psum(partial_innovation, ('row', 'col')) + jnp.diag(sensor_noise)  125 us
    another operation x11, other arithmetic, shards(): lower = jnp.linalg.cholesky(symmetric)  57.2 us
    ppermute x8, waiting for transfers between devices, column_rows(): pieces.append(lax.ppermute(local_rows, ('row', 'col'), perm))  36.4 us
    unnamed x109, local copies, waits for them, and re-layouts  33.1 us
    another operation x3, other arithmetic, shards(): jax.scipy.linalg.solve_triangular(lower, jnp.eye(sensors, dtype=jnp.float...  29.5 us
    dot_general x1, matrix products, shards(): jnp.dot(predicted, col_observe.T, precision=lax.Precision.HIGHEST)  29.1 us
    psum x1, waiting for transfers between devices, shards(): cross_cov = lax.psum(partial_cross, 'col')  27.8 us
    dot_general x16, matrix products, dot_f32(): lax.dot_general(a, b, (dims, ((), ())), preferred_element_type=jnp.float32)  27.6 us
  transfers between devices with their start and end apart: 19, of which 13 were waited for; matrix products, arithmetic and copies ran while one was open for 21% of the time, Pallas kernels for 0%

profile of v3, /device:TPU:27, one launch (start us, length us, event | category | flops | bytes accessed | tf_op | source)
XLA Modules:
  0.0 562.6 jit_solution(3208383284402310060)
XLA Ops:
  32.9 8.7 %fusion = (bf16[4,512,1024]{2,1,0:T(8,128)(2,1)}, bf16[4,512,1024]{2,1,0:T(8,128)(2,1)}) fusion(f32[4,512,1024]{2,1,0:T(8,128)} %bitcast.269), kind=kLoop, calls=%fused_computation.7 | loop fusion | flops 8388608 | bytes 16777216 | tf_op jit(solution)/shard_map/convert_element_type | solution.py:60
  73.8 20.5 %all-gather.3.cloned.1.call-done = bf16[16,128,1024]{2,1,0:T(8,128)(2,1)} async-done(((bf16[4,128,1024]{2,1,0:T(8,128)(2,1)}), bf16[16,128,1024]{2,1,0:T(8,128)(2,1)}) %all-gather.3.cloned.1.call-update) | async-done | bytes 4194320 | tf_op jit(solution)/shard_map/all_gather | solution.py:112
  110.3 4.7 collective-permute-start.8
  130.0 5.9 %collective-permute-done.8 = bf16[256,512]{1,0:T(8,128)(2,1)S(1)} collective-permute-done((bf16[256,512]{1,0:T(8,128)(2,1)S(1)}, bf16[256,512]{1,0:T(8,128)(2,1)S(1)}, u32[]{:S(2)}, u32[]{:S(2)}) %collective-permute-start.8) | collective-permute-done | bytes 262176 | tf_op jit(solution)/shard_map/ppermute | solution.py:70
  151.4 21.8 %all-gather.5.cloned.1.call-done = bf16[16,2048,128]{2,1,0:T(8,128)(2,1)} async-done(((bf16[2,2048,128]{2,1,0:T(8,128)(2,1)}), bf16[16,2048,128]{2,1,0:T(8,128)(2,1)}) %all-gather.5.cloned.1.call-update) | async-done | bytes 8388624 | tf_op jit(solution)/shard_map/all_gather | solution.py:132
  173.2 6.6 %fusion.10 = f32[2048,128]{0,1:T(8,128)S(1)} fusion(bf16[16,2048,128]{2,1,0:T(8,128)(2,1)} %all-gather.5.cloned.1.call-done, f32[2048,512]{0,1:T(8,128)} %copy-done.1, pred[16]{0:T(512)(128)(4,1)S(1)} %iota_compare_fusion.9, pred[16]{0:T(512)(128)(4,1)S(1)} %iota_compare_fusion.10, pred[16]{0:T(512)(128)(4,1)S(1)} %iota_compare_fusion.11, ...), kind=kOutput, calls=%fused_computation.21 | convolution fusion | flops 1076101120 | bytes 10616897 | tf_op jit(solution)/shard_map/dot_general | solution.py:89
  179.9 4.5 fusion.9
  185.4 29.1 %fusion.18 = f32[2048,384]{1,0:T(8,128)} fusion(f32[384,1024]{1,0:T(8,128)S(1)} %bitcast.286, f32[384]{0:T(512)S(1)} %get-tuple-element.109, f32[384]{0:T(512)S(1)} %get-tuple-element.108, s32[1024]{0:T(1024)S(1)} %get-tuple-element.110, s32[384]{0:T(512)S(1)} %copy-done.29, pred[1024]{0:T(1024)(128)(4,1)S(1)} %get-tuple-element.112, ...), kind=kOutput, calls=%fused_computation.43 | convolution fusion | flops 9678225408 | bytes 13134336 | tf_op jit(solution)/shard_map/dot_general | solution.py:159
  214.5 9.5 %fusion.1 = f32[384,384]{0,1:T(8,128)} fusion(f32[2048,384]{1,0:T(8,128)} %fusion.18, f32[384,2048]{1,0:T(8,128)} %bitcast.279, f32[384]{0:T(512)S(1)} %get-tuple-element.109, f32[384]{0:T(512)S(1)} %get-tuple-element.108, s32[2048]{0:T(1024)S(1)} %get-tuple-element.128, s32[384]{0:T(512)S(1)} %copy-done.29, pred[2048]{0:T(1024)(128)(4,1)S(1)} %get-tuple-element.114, ...), kind=kOutput, calls=%fused_computation.10 | convolution fusion | flops 3627810816 | bytes 6898176 | tf_op jit(solution)/shard_map/dot_general | solution.py:163
  224.2 125.3 %all-reduce.4.cloned.1.call-done = f32[384,384]{0,1:T(8,128)} async-done(((f32[384,384]{0,1:T(8,128)}), f32[384,384]{0,1:T(8,128)}) %all-reduce.4.cloned.1.call-update) | async-done | bytes 589840 | tf_op jit(solution)/shard_map/psum | solution.py:164
  351.2 11.7 %cholesky.76 = f32[128,128]{1,0:T(8,128)S(1)} custom-call(f32[128,128]{1,0:T(8,128)S(1)} %cholesky.189), custom_call_target="Cholesky" | custom-call | tf_op jit(solution)/shard_map/jit(cholesky)/cholesky | solution.py:168
  363.0 9.8 %custom-call.23 = f32[1,128,128]{1,2,0:T(8,128)S(1)} custom-call(f32[1,128,128]{2,1,0:T(8,128)S(1)} %get-tuple-element.77), custom_call_target="InvertDiagBlocksLowerTriangular" | custom-call | tf_op jit(solution)/shard_map/jit(cholesky)/cholesky | solution.py:168
  373.3 11.7 %cholesky.160 = f32[128,128]{1,0:T(8,128)S(1)} custom-call(f32[128,128]{1,0:T(8,128)S(1)} %cholesky.193), custom_call_target="Cholesky" | custom-call | tf_op jit(solution)/shard_map/jit(cholesky)/cholesky | solution.py:168
  385.4 10.2 %custom-call.24 = f32[1,128,128]{1,2,0:T(8,128)S(1)} custom-call(f32[1,128,128]{2,1,0:T(8,128)S(1)} %get-tuple-element.75), custom_call_target="InvertDiagBlocksLowerTriangular" | custom-call | tf_op jit(solution)/shard_map/jit(cholesky)/cholesky | solution.py:168
  396.3 11.7 %cholesky.179 = f32[128,128]{1,0:T(8,128)S(1)} custom-call(f32[128,128]{1,0:T(8,128)S(1)} %convolution_subtract_fusion.4), custom_call_target="Cholesky" | custom-call | tf_op jit(solution)/shard_map/jit(cholesky)/cholesky | solution.py:168
  412.2 6.3 %while.1 = (s32[]{:T(128)}, f32[384,384]{0,1:T(8,128)S(1)}, s32[3,2]{0,1:T(2,128)S(1)}, f32[3,128,128]{2,1,0:T(8,128)S(1)}, s32[]{:T(128)}) while((s32[]{:T(128)}, f32[384,384]{0,1:T(8,128)S(1)}, s32[3,2]{0,1:T(2,128)S(1)}, f32[3,128,128]{2,1,0:T(8,128)S(1)}, s32[]{:T(128)}) %tuple.101), condition=%wide.while_cond, body=%wide.while_body.sunk | while | flops 2 | bytes 393321 | solution.py:170
  418.6 29.5 %custom-call.25 = f32[3,128,128]{1,2,0:T(8,128)S(1)} custom-call(f32[3,128,128]{2,1,0:T(8,128)S(1)} %get-tuple-element.13), custom_call_target="InvertDiagBlocksLowerTriangular" | custom-call | tf_op jit(solution)/shard_map/jit(_solve_triangular)/triangular_solve | solution.py:170
  451.8 27.8 %all-reduce.6.cloned.1.call-done = f32[2048,384]{1,0:T(8,128)} async-done(((f32[2048,384]{1,0:T(8,128)}), f32[2048,384]{1,0:T(8,128)}) %all-reduce.6.cloned.1.call-update) | async-done | bytes 3145744 | tf_op jit(solution)/shard_map/psum | solution.py:166
  492.2 7.2 %fusion.213 = f32[2048,384]{0,1:T(8,128)S(1)} fusion(f32[2048,384]{1,0:T(8,128)} %all-reduce.6.cloned.1.call-done, f32[384,384]{1,0:T(8,128)S(1)} %fusion.47), kind=kOutput, calls=%fused_computation.395 | convolution fusion | flops 3623878656 | bytes 6881280 | tf_op jit(solution)/shard_map/dot_general | solution.py:174
  500.3 10.7 %collective-permute-done.11 = f32[256,384]{1,0:T(8,128)S(1)} collective-permute-done((f32[256,384]{1,0:T(8,128)S(1)}, f32[256,384]{1,0:T(8,128)S(1)}, u32[]{:S(2)}, u32[]{:S(2)}) %collective-permute-start.11) | collective-permute-done | bytes 393248 | tf_op jit(solution)/shard_map/ppermute | solution.py:70
  511.0 10.0 %collective-permute-done.12 = f32[256,384]{1,0:T(8,128)S(1)} collective-permute-done((f32[256,384]{1,0:T(8,128)S(1)}, f32[256,384]{1,0:T(8,128)S(1)}, u32[]{:S(2)}, u32[]{:S(2)}) %collective-permute-start.12) | collective-permute-done | bytes 393248 | tf_op jit(solution)/shard_map/ppermute | solution.py:70
  521.0 5.5 collective-permute-done.13
  529.4 17.2 %convolution_subtract_fusion = f32[2048,1024]{0,1:T(8,128)} fusion(f32[2048,384]{0,1:T(8,128)S(1)} %copy-done.7, f32[1024,384]{1,0:T(8,128)S(1)} %bitcast_select_fusion, f32[1024]{0:T(1024)S(1)} %copy-done.33, s32[1024]{0:T(1024)S(1)} %get-tuple-element.111, s32[2048]{0:T(1024)S(1)} %get-tuple-element.129, f32[2048,384]{0,1:T(8,128)} %slice.396, ...), kind=kOutput, calls=%fused_computation.9 | convolution fusion | flops 9678356480 | bytes 21512192 | tf_op jit(solution)/shard_map/dot_general | solution.py:178
  546.6 9.2 %copy.69 = f32[2048,1024]{1,0:T(8,128)} copy(f32[2048,1024]{0,1:T(8,128)} %convolution_subtract_fusion) | data formatting | bytes 16777216
  (274 shorter events, 136.5 us)
Async XLA Ops:
  7.2 25.0 %copy-start.18 = (bf16[256,512]{1,0:T(8,128)(2,1)S(1)}, bf16[256,512]{1,0:T(8,128)(2,1)}, u32[]{:S(2)}) copy-start(bf16[256,512]{1,0:T(8,128)(2,1)} %param.10) | copy-start | bytes 786436
  7.2 87.2 %all-gather.3.cloned.1.call-start = ((), (), s32[]{:S(2)}) async-start(), calls=%async_computation | async-start | bytes 5242880 | tf_op jit(solution)/shard_map/all_gather | solution.py:112
  7.2 38.7 %collective-permute-start = (bf16[256,512]{1,0:T(8,128)(2,1)}, bf16[256,512]{1,0:T(8,128)(2,1)S(1)}, u32[]{:S(2)}, u32[]{:S(2)}) collective-permute-start(bf16[256,512]{1,0:T(8,128)(2,1)} %param.10), channel_id=1, source_target_pairs={{0,1},{1,2},{2,3},{3,4},{4,5},{5,6},{6,7},{7,0},{8,9},{9,10},{10,1... | collective-permute-start | bytes 786440 | tf_op jit(solution)/shard_map/ppermute | solution.py:52
  9.1 38.8 %collective-permute-start.1 = (bf16[256,512]{1,0:T(8,128)(2,1)}, bf16[256,512]{1,0:T(8,128)(2,1)S(1)}, u32[]{:S(2)}, u32[]{:S(2)}) collective-permute-start(bf16[256,512]{1,0:T(8,128)(2,1)} %param.10), channel_id=1, source_target_pairs={{0,2},{1,3},{2,4},{3,5},{4,6},{5,7},{6,0},{7,1},{8,10},{9,11},{10,... | collective-permute-start | bytes 786440 | tf_op jit(solution)/shard_map/ppermute | solution.py:52
  10.3 38.3 %collective-permute-start.2 = (bf16[256,512]{1,0:T(8,128)(2,1)}, bf16[256,512]{1,0:T(8,128)(2,1)S(1)}, u32[]{:S(2)}, u32[]{:S(2)}) collective-permute-start(bf16[256,512]{1,0:T(8,128)(2,1)} %param.10), channel_id=1, source_target_pairs={{0,3},{1,4},{2,5},{3,6},{4,7},{5,0},{6,1},{7,2},{8,11},{9,12},{10,... | collective-permute-start | bytes 786440 | tf_op jit(solution)/shard_map/ppermute | solution.py:52
  10.3 39.0 %collective-permute-start.3 = (bf16[256,512]{1,0:T(8,128)(2,1)}, bf16[256,512]{1,0:T(8,128)(2,1)S(1)}, u32[]{:S(2)}, u32[]{:S(2)}) collective-permute-start(bf16[256,512]{1,0:T(8,128)(2,1)} %param.10), channel_id=1, source_target_pairs={{0,4},{1,5},{2,6},{3,7},{4,0},{5,1},{6,2},{7,3},{8,12},{9,13},{10,... | collective-permute-start | bytes 786440 | tf_op jit(solution)/shard_map/ppermute | solution.py:52
  10.9 39.2 %collective-permute-start.4 = (bf16[256,512]{1,0:T(8,128)(2,1)}, bf16[256,512]{1,0:T(8,128)(2,1)S(1)}, u32[]{:S(2)}, u32[]{:S(2)}) collective-permute-start(bf16[256,512]{1,0:T(8,128)(2,1)} %param.10), channel_id=1, source_target_pairs={{0,5},{1,6},{2,7},{3,0},{4,1},{5,2},{6,3},{7,4},{8,13},{9,14},{10,... | collective-permute-start | bytes 786440 | tf_op jit(solution)/shard_map/ppermute | solution.py:52
  15.3 158.0 %all-gather.5.cloned.1.call-start = ((), (), s32[]{:S(2)}) async-start(), calls=%async_computation.1 | async-start | bytes 9437184 | tf_op jit(solution)/shard_map/all_gather | solution.py:132
  45.9 9.1 %collective-permute-start.5 = (bf16[256,512]{1,0:T(8,128)(2,1)S(1)}, bf16[256,512]{1,0:T(8,128)(2,1)S(1)}, u32[]{:S(2)}, u32[]{:S(2)}) collective-permute-start(bf16[256,512]{1,0:T(8,128)(2,1)S(1)} %copy-done.18), channel_id=1, source_target_pairs={{0,6},{1,7},{2,0},{3,1},{4,2},{5,3},{6,4},{7,5},{8,14},{9,15},{10,... | collective-permute-start | bytes 786440 | tf_op jit(solution)/shard_map/ppermute | solution.py:52
  47.8 10.2 %collective-permute-start.6 = (bf16[256,512]{1,0:T(8,128)(2,1)S(1)}, bf16[256,512]{1,0:T(8,128)(2,1)S(1)}, u32[]{:S(2)}, u32[]{:S(2)}) collective-permute-start(bf16[256,512]{1,0:T(8,128)(2,1)S(1)} %copy-done.18), channel_id=1, source_target_pairs={{0,7},{1,0},{2,1},{3,2},{4,3},{5,4},{6,5},{7,6},{8,15},{9,8},{10,9... | collective-permute-start | bytes 786440 | tf_op jit(solution)/shard_map/ppermute | solution.py:52
  103.5 20.7 %copy-start.16 = (f32[384,512]{1,0:T(8,128)S(1)}, f32[384,512]{1,0:T(8,128)}, u32[]{:S(2)}) copy-start(f32[384,512]{1,0:T(8,128)} %param.16) | copy-start | bytes 2359300
  106.8 242.7 %all-reduce.4.cloned.1.call-start = ((), (), s32[]{:S(2)}) async-start(), calls=%async_computation.2 | async-start | bytes 1179648 | tf_op jit(solution)/shard_map/psum | solution.py:164
  106.9 23.1 %collective-permute-start.7 = (bf16[256,512]{1,0:T(8,128)(2,1)S(1)}, bf16[256,512]{1,0:T(8,128)(2,1)S(1)}, u32[]{:S(2)}, u32[]{:S(2)}) collective-permute-start(bf16[256,512]{1,0:T(8,128)(2,1)S(1)} %copy-done.18), channel_id=1, source_target_pairs={{0,0},{1,8},{2,16},{3,24},{4,1},{5,9},{6,17},{7,25},{8,2},{9,10},{... | collective-permute-start | bytes 786440 | tf_op jit(solution)/shard_map/ppermute | solution.py:70
  110.3 25.6 %collective-permute-start.8 = (bf16[256,512]{1,0:T(8,128)(2,1)S(1)}, bf16[256,512]{1,0:T(8,128)(2,1)S(1)}, u32[]{:S(2)}, u32[]{:S(2)}) collective-permute-start(bf16[256,512]{1,0:T(8,128)(2,1)S(1)} %copy-done.18), channel_id=1, source_target_pairs={{0,8},{1,16},{2,24},{3,0},{4,9},{5,17},{6,25},{7,1},{8,10},{9,18},... | collective-permute-start | bytes 786440 | tf_op jit(solution)/shard_map/ppermute | solution.py:70
  115.0 23.6 %collective-permute-start.9 = (bf16[256,512]{1,0:T(8,128)(2,1)S(1)}, bf16[256,512]{1,0:T(8,128)(2,1)S(1)}, u32[]{:S(2)}, u32[]{:S(2)}) collective-permute-start(bf16[256,512]{1,0:T(8,128)(2,1)S(1)} %copy-done.18), channel_id=1, source_target_pairs={{0,16},{1,24},{2,0},{3,8},{4,17},{5,25},{6,1},{7,9},{8,18},{9,26},... | collective-permute-start | bytes 786440 | tf_op jit(solution)/shard_map/ppermute | solution.py:70
  116.0 23.8 %collective-permute-start.10 = (bf16[256,512]{1,0:T(8,128)(2,1)S(1)}, bf16[256,512]{1,0:T(8,128)(2,1)S(1)}, u32[]{:S(2)}, u32[]{:S(2)}) collective-permute-start(bf16[256,512]{1,0:T(8,128)(2,1)S(1)} %copy-done.18), channel_id=1, source_target_pairs={{0,24},{1,0},{2,8},{3,16},{4,25},{5,1},{6,9},{7,17},{8,26},{9,2},{... | collective-permute-start | bytes 786440 | tf_op jit(solution)/shard_map/ppermute | solution.py:70
  146.2 38.2 %copy-start.11 = (f32[2048,384]{0,1:T(8,128)}, f32[2048,384]{0,1:T(8,128)S(1)}, u32[]{:S(2)}) copy-start(f32[2048,384]{0,1:T(8,128)S(1)} %slice.392) | copy-start | bytes 9437188
  214.5 135.0 %copy-start.28 = (f32[384]{0:T(512)S(1)}, f32[384]{0:T(512)}, u32[]{:S(2)}) copy-start(f32[384]{0:T(512)} %param.17) | copy-start | bytes 4612
  224.0 255.6 %all-reduce.6.cloned.1.call-start = ((), (), s32[]{:S(2)}) async-start(), calls=%async_computation.3 | async-start | bytes 6291456 | tf_op jit(solution)/shard_map/psum | solution.py:166
  480.6 30.4 %collective-permute-start.11 = (f32[256,384]{1,0:T(8,128)S(1)}, f32[256,384]{1,0:T(8,128)S(1)}, u32[]{:S(2)}, u32[]{:S(2)}) collective-permute-start(f32[256,384]{1,0:T(8,128)S(1)} %constant_dynamic-slice_fusion.2), channel_id=1, source_target_pairs={{0,0},{1,8},{2,16},{3,24},{4,1},{5,9},{6,17},{7,25},{8,2},{9,10},{... | collective-permute-start | bytes 1179656 | tf_op jit(solution)/shard_map/ppermute | solution.py:70
  483.6 37.4 %collective-permute-start.12 = (f32[256,384]{1,0:T(8,128)S(1)}, f32[256,384]{1,0:T(8,128)S(1)}, u32[]{:S(2)}, u32[]{:S(2)}) collective-permute-start(f32[256,384]{1,0:T(8,128)S(1)} %constant_dynamic-slice_fusion.2), channel_id=1, source_target_pairs={{0,8},{1,16},{2,24},{3,0},{4,9},{5,17},{6,25},{7,1},{8,10},{9,18},... | collective-permute-start | bytes 1179656 | tf_op jit(solution)/shard_map/ppermute | solution.py:70
  487.9 38.5 %collective-permute-start.13 = (f32[256,384]{1,0:T(8,128)S(1)}, f32[256,384]{1,0:T(8,128)S(1)}, u32[]{:S(2)}, u32[]{:S(2)}) collective-permute-start(f32[256,384]{1,0:T(8,128)S(1)} %constant_dynamic-slice_fusion.2), channel_id=1, source_target_pairs={{0,16},{1,24},{2,0},{3,8},{4,17},{5,25},{6,1},{7,9},{8,18},{9,26},... | collective-permute-start | bytes 1179656 | tf_op jit(solution)/shard_map/ppermute | solution.py:70
  489.1 37.7 %collective-permute-start.14 = (f32[256,384]{1,0:T(8,128)S(1)}, f32[256,384]{1,0:T(8,128)S(1)}, u32[]{:S(2)}, u32[]{:S(2)}) collective-permute-start(f32[256,384]{1,0:T(8,128)S(1)} %constant_dynamic-slice_fusion.2), channel_id=1, source_target_pairs={{0,24},{1,0},{2,8},{3,16},{4,25},{5,1},{6,9},{7,17},{8,26},{9,2},{... | collective-permute-start | bytes 1179656 | tf_op jit(solution)/shard_map/ppermute | solution.py:70
  499.4 27.3 %copy-start.6 = (f32[2048,384]{0,1:T(8,128)}, f32[2048,384]{0,1:T(8,128)S(1)}, u32[]{:S(2)}) copy-start(f32[2048,384]{0,1:T(8,128)S(1)} %fusion.213) | copy-start | bytes 9437188
  (41 other events, 161.8 us)
Sparse Core Ops, SparseCore 0:
  15.4 78.9 all-gather.2
  106.9 66.2 all-gather.4
  224.1 125.3 all-reduce.3
  408.3 71.1 all-reduce.5
